TPU v7x, 256 devices: a whole 4x4x8 slice. The times are simulated.
256 devices in a mesh: ctx: 16 (over y_lo, z), dp: 16 (over x, y_hi, core).
Axes of the slice: x: 4, y: 4 (y_hi: 2, y_lo: 2; y = y_hi * 2 + y_lo), z: 8, core: 2. Of those that a mesh axis runs over, the one named last changes fastest.
Arguments:
- queries: bfloat16 [16, 4096, 2048], P('dp', 'ctx'), may hold values from -9 to 9, as said below
- keys: bfloat16 [16, 4096, 512], P('dp', 'ctx'), may hold values from -9 to 9
- values: bfloat16 [16, 4096, 512], P('dp', 'ctx'), may hold values from -20 to 20
- hyena_x1: bfloat16 [16, 4096, 2048], P('dp', 'ctx'), may hold values from -6 to 6
- hyena_x2: bfloat16 [16, 4096, 2048], P('dp', 'ctx'), may hold values from -6 to 6
- hyena_v: bfloat16 [16, 4096, 2048], P('dp', 'ctx'), may hold values from -6 to 6
- filters: bfloat16 [128, 128], replicated, may hold values from -6 to 6
- panels: bfloat16 [16, 512, 4096], P('dp', 'ctx'), may hold values from -6 to 6
- owner: int32 [16, 512, 1], P('dp', 'ctx'), may hold values from 0 to 15; in each aligned block of 32 rows (0 to 31, 32 to 63, ..., all dimensions but the last counted through in order) at most 8 rows name the same one
- step_rows: int32 [16, 512], P('dp', 'ctx'), may hold values from 0 to 4095, as said below
Outputs:
- mixed: bfloat16 [16, 4096, 2048], P('dp', 'ctx')
Inputs may be any that keep to these rules, and one draw needn't show every extreme that they name: In the hidden draw a few queries are aligned with two earlier keys; the normal draw stays within 6. `step_rows`: the panels held by the device at index c of ctx belong to positions c * 256 to (c + 1) * 256 - 1 of their traces. Of the panels on one device, at most 8 have the same owner, and that bound is reached.
All inputs are finite; a program needn't handle non-finite values.
Results may differ from a plain program's by a relative error of at most 0.0055.
Values may be sent and summed in bfloat16 or wider, within the bound.
No kernel may reach another device: no remote copies, remote signals or barrier semaphores. Data moves between devices by JAX's collectives and lax.ppermute only.
A program may use at most 128 MiB of HBM per device.

v0:
```python
import functools

import jax
import jax.numpy as jnp
from jax import lax
from jax.sharding import PartitionSpec as P
from jax.experimental import pallas as pl
from jax.experimental.pallas import tpu as pltpu

HEADS = 16
KV_HEADS = 4
HEAD_DIM = 128


NEG = -1e30


def passed_along(block, axis, distance):
    devices = range(lax.axis_size(axis))
    route = [(i - distance, i) for i in devices if i - distance in devices]
    return lax.ppermute(block, axis, route)


ROW = 8


def flash_kernel(first, final, count, *refs):
    flags_ref, q_ref = refs[0], refs[1]
    at = 2
    if not first:
        m_in, l_in, acc_in = refs[at : at + 3]
        at += 3
    kv_refs = refs[at : at + count]
    at += count
    outs = refs[at : at + (1 if final else 3)]
    qs_sc, m_sc, l_sc, acc_sc = refs[at + len(outs) :]
    grp = HEADS // KV_HEADS
    tok = q_ref.shape[0]
    scale = HEAD_DIM ** (-0.5)

    for g in range(KV_HEADS):
        for j in range(grp):
            col = (g * grp + j) * HEAD_DIM
            qs_sc[g, j * tok : (j + 1) * tok, :] = q_ref[:, col : col + HEAD_DIM]
    if first:
        m_sc[...] = jnp.full_like(m_sc, NEG)
        l_sc[...] = jnp.zeros_like(l_sc)
        acc_sc[...] = jnp.zeros_like(acc_sc)
    else:
        m_sc[...] = m_in[...]
        l_sc[...] = l_in[...]
        acc_sc[...] = acc_in[...]

    def update(kv_ref, masked):
        def one(g, carry):
            k = kv_ref[g]
            v = kv_ref[KV_HEADS + g]
            s = lax.dot_general(
                k, qs_sc[g], (((1,), (1,)), ((), ())), preferred_element_type=jnp.float32
            ) * scale
            if masked:
                rows = lax.broadcasted_iota(jnp.int32, s.shape, 0)
                cols = lax.broadcasted_iota(jnp.int32, s.shape, 1) % tok
                s = jnp.where(rows <= cols, s, NEG)
            m_old = m_sc[g]
            m_new = jnp.maximum(m_old, jnp.max(s, axis=0, keepdims=True))
            p = jnp.exp(s - m_new)
            alpha = jnp.exp(m_old - m_new)
            l_sc[g] = alpha * l_sc[g] + jnp.sum(p, axis=0, keepdims=True)
            pv = lax.dot_general(
                v, p.astype(jnp.bfloat16), (((0,), (0,)), ((), ())),
                preferred_element_type=jnp.float32,
            )
            acc_sc[g] = alpha * acc_sc[g] + pv
            m_sc[g] = m_new
            return carry

        lax.fori_loop(0, KV_HEADS, one, 0)

    for i in range(count):
        if first and i == 0:
            update(kv_refs[0], True)
            continue

        @pl.when(flags_ref[i] > 0)
        def _(i=i):
            update(kv_refs[i], False)

    if final:
        o_ref = outs[0]
        for g in range(KV_HEADS):
            normed = acc_sc[g] / l_sc[g]
            for j in range(grp):
                col = (g * grp + j) * HEAD_DIM
                o_ref[:, col : col + HEAD_DIM] = normed[:, j * tok : (j + 1) * tok].T
    else:
        outs[0][...] = m_sc[...]
        outs[1][...] = l_sc[...]
        outs[2][...] = acc_sc[...]


def flash(flags, query, blocks, state, final):
    tok = query.shape[0]
    grp = HEADS // KV_HEADS
    vmem = pl.BlockSpec(memory_space=pltpu.VMEM)
    stat = jax.ShapeDtypeStruct((KV_HEADS, 1, grp * tok), jnp.float32)
    acc = jax.ShapeDtypeStruct((KV_HEADS, HEAD_DIM, grp * tok), jnp.float32)
    if final:
        out_shape = jax.ShapeDtypeStruct((tok, HEADS * HEAD_DIM), jnp.float32)
        out_specs = vmem
    else:
        out_shape = (stat, stat, acc)
        out_specs = (vmem, vmem, vmem)
    first = state is None
    extra = () if first else tuple(state)
    kernel = functools.partial(flash_kernel, first, final, len(blocks))
    return pl.pallas_call(
        kernel,
        out_shape=out_shape,
        in_specs=[pl.BlockSpec(memory_space=pltpu.SMEM)]
        + [vmem] * (1 + len(extra) + len(blocks)),
        out_specs=out_specs,
        scratch_shapes=[
            pltpu.VMEM((KV_HEADS, grp * tok, HEAD_DIM), jnp.bfloat16),
            pltpu.VMEM((KV_HEADS, 1, grp * tok), jnp.float32),
            pltpu.VMEM((KV_HEADS, 1, grp * tok), jnp.float32),
            pltpu.VMEM((KV_HEADS, HEAD_DIM, grp * tok), jnp.float32),
        ],
        compiler_params=pltpu.CompilerParams(vmem_limit_bytes=48 * 1024 * 1024),
    )(flags, query, *extra, *blocks)


def attention(query, key_rows, val_rows, tok, ctx_index):
    count = lax.axis_size("ctx")
    rows = count // ROW
    kv = jnp.concatenate([key_rows, val_rows], axis=1)
    kv = kv.reshape(tok, 2 * KV_HEADS, HEAD_DIM).transpose(1, 0, 2)
    plus = [(r * ROW + z, r * ROW + (z + 1) % ROW) for r in range(rows) for z in range(ROW)]
    minus = [(r * ROW + z, r * ROW + (z - 1) % ROW) for r in range(rows) for z in range(ROW)]
    lefts, rights = [kv], [kv]
    for _ in range(ROW // 2):
        lefts.append(lax.ppermute(lefts[-1], "ctx", plus))
    for _ in range(ROW - 1 - ROW // 2):
        rights.append(lax.ppermute(rights[-1], "ctx", minus))
    row_blocks = [kv]
    for k in range(1, max(len(lefts), len(rights))):
        row_blocks += [side[k] for side in (lefts, rights) if k < len(side)]
    z = ctx_index % ROW
    r = ctx_index // ROW
    flags = [jnp.int32(1)]
    for k in range(1, max(len(lefts), len(rights))):
        if k < len(lefts):
            flags.append((z - k >= 0).astype(jnp.int32))
        if k < len(rights):
            flags.append((z + k >= ROW).astype(jnp.int32))
    blocks = list(row_blocks)
    for lower in range(rows - 1):
        for upper in range(lower + 1, rows):
            up = [(lower * ROW + z2, upper * ROW + z2) for z2 in range(ROW)]
            for piece in row_blocks:
                blocks.append(lax.ppermute(piece, "ctx", up))
                flags.append((r == upper).astype(jnp.int32))
    split = len(row_blocks)
    if split == len(blocks):
        return flash(jnp.stack(flags), query, blocks, None, True)
    state = flash(jnp.stack(flags[:split]), query, blocks[:split], None, False)
    late = split + len(row_blocks) - 3
    state = flash(jnp.stack(flags[split:late]), query, blocks[split:late], state, False)
    return flash(jnp.stack(flags[late:]), query, blocks[late:], state, True)


def hyena_conv(first_in, value_in, filters, tok):
    width = first_in.shape[1]
    taps = filters.shape[1]
    fgroups = filters.shape[0]
    u_rows = (first_in.astype(jnp.float32) * value_in.astype(jnp.float32)).astype(jnp.bfloat16)
    before = passed_along(u_rows[tok - taps :], "ctx", 1)
    return conv_body(before, u_rows, filters, tok, width, taps, fgroups)


def conv_body(before, u_rows, filters, tok, width, taps, fgroups):
    extended = jnp.concatenate([before, u_rows], 0)
    nblk = tok // taps
    blocks = extended.reshape(nblk + 1, taps, fgroups, width // fgroups)
    rows_at = jnp.arange(taps, dtype=jnp.int32)
    lag = rows_at[:, None] - rows_at[None, :]
    wrapped = (lag + taps) % taps
    selector = (wrapped[None, :, :] == rows_at[:, None, None]).astype(jnp.bfloat16)
    circulant = jnp.einsum(
        "gk,kij->gij", filters, selector, preferred_element_type=jnp.float32
    ).astype(jnp.bfloat16)
    nothing = jnp.zeros((), jnp.bfloat16)
    lower = jnp.where((lag >= 0)[None], circulant, nothing)
    upper = jnp.where((lag < 0)[None], circulant, nothing)
    conv = jnp.einsum("gij,bjgc->bigc", lower, blocks[1:], preferred_element_type=jnp.float32)
    conv = conv + jnp.einsum(
        "gij,bjgc->bigc", upper, blocks[:-1], preferred_element_type=jnp.float32
    )
    return conv.reshape(tok, width)


def blend(rows, width):
    gates = rows[:, :width].astype(jnp.float32)
    vals = rows[:, width:].astype(jnp.float32)
    return (jax.nn.sigmoid(gates) * vals).astype(jnp.bfloat16)


def place_rows(slots, rows, total_slots):
    placing = (jnp.arange(total_slots, dtype=jnp.int32)[:, None] == slots[None, :]).astype(
        jnp.bfloat16
    )
    return jnp.dot(placing, rows, preferred_element_type=jnp.float32).astype(jnp.bfloat16)


def route_hints(panels, owner, step_rows, width, tok, ctx_index):
    dp_count = lax.axis_size("dp")
    count = panels.shape[1]
    entries = panels.shape[2]
    cap = min(count, 4 * count // dp_count)
    owners = owner[0, :, 0]
    marks = (owners[:, None] == jnp.arange(dp_count, dtype=jnp.int32)[None, :]).astype(jnp.int32)
    before_mask = (
        jnp.arange(count, dtype=jnp.int32)[:, None] > jnp.arange(count, dtype=jnp.int32)[None, :]
    ).astype(jnp.int32)
    earlier = jnp.sum(jnp.dot(before_mask, marks) * marks, axis=1)
    slots = owners * cap + earlier
    base_row = ctx_index * tok
    row_buffer = jnp.full((dp_count * cap,), base_row, jnp.int32).at[slots].set(step_rows[0])
    arrived_rows = (
        lax.all_to_all(
            row_buffer.reshape(dp_count, cap), "dp", split_axis=0, concat_axis=0, tiled=True
        ).reshape(dp_count * cap)
        - base_row
    )
    buffer = place_rows(slots, panels[0], dp_count * cap)
    received = lax.all_to_all(
        buffer.reshape(dp_count, cap, entries), "dp", split_axis=0, concat_axis=0, tiled=True
    )
    arrived = blend(received.reshape(dp_count * cap, entries), width)
    landing = (jnp.arange(tok, dtype=jnp.int32)[:, None] == arrived_rows[None, :]).astype(
        jnp.bfloat16
    )
    return jnp.dot(landing, arrived, preferred_element_type=jnp.float32)


def per_device(
    queries, keys, values, hyena_x1, hyena_x2, hyena_v, filters, panels, owner, step_rows
):
    tok = queries.shape[1]
    width = hyena_x1.shape[2]
    ctx_index = lax.axis_index("ctx")
    conv = hyena_conv(hyena_x1[0], hyena_v[0], filters, tok)
    attended = attention(queries[0], keys[0], values[0], tok, ctx_index)
    hints = route_hints(panels, owner, step_rows, width, tok, ctx_index)
    total = hyena_x2[0].astype(jnp.float32) * conv + attended + hints
    return total.astype(jnp.bfloat16)[None]


def solution(mesh):
    placed = (
        P("dp", "ctx", None),
        P("dp", "ctx", None),
        P("dp", "ctx", None),
        P("dp", "ctx", None),
        P("dp", "ctx", None),
        P("dp", "ctx", None),
        P(),
        P("dp", "ctx", None),
        P("dp", "ctx", None),
        P("dp", "ctx"),
    )
    return jax.shard_map(
        per_device, mesh=mesh, in_specs=placed, out_specs=P("dp", "ctx", None), check_vma=False
    )
```

profile of v0, /device:TPU:234, one launch (start us, length us, event | category | flops | bytes accessed | tf_op | source)
XLA Modules:
  0.0 174.5 jit_solution(15898660172085187023)
XLA Ops:
  0.0 1.1 copy.35
  1.1 0.2 copy.37
  1.3 1.1 copy.36
  2.4 0.2 copy.38
  2.8 2.0 %collective-permute-start.2 = (bf16[8,256,128]{2,1,0:T(8,128)(2,1)S(1)}, bf16[8,256,128]{2,1,0:T(8,128)(2,1)S(1)}, u32[]{:S(2)}, u32[]{:S(2)}) collective-permute-start(bf16[8,256,128]{2,1,0:T(8,128)(2,1)S(1)} %maximum_bitcast_fusion.refs_2_), channel_id=1, source_target_pairs={{0,112},{16,0},{32,16},{48,32},{64,48},{80,64},{96,80},{112,96},{1... | collective-permute-start | bytes 1572872 | tf_op jit(solution)/shard_map/ppermute | solution.py:144
  4.8 1.3 collective-permute-start.8
  6.1 1.9 %multiply_convert_fusion = bf16[1,256,2048]{2,1,0:T(8,128)(2,1)S(1)} fusion(bf16[1,256,2048]{2,1,0:T(8,128)(2,1)} %param.15, bf16[1,256,2048]{2,1,0:T(8,128)(2,1)} %param.13), kind=kLoop, calls=%fused_computation.15 | loop fusion | flops 2097152 | bytes 3145728 | tf_op jit(solution)/shard_map/convert_element_type | solution.py:176
  8.0 0.9 slice_bitcast_fusion
  8.9 1.3 collective-permute-start
  10.2 0.1 fusion.7
  10.4 7.3 %collective-permute-done.1.refs_3_ = bf16[8,256,128]{2,1,0:T(8,128)(2,1)} collective-permute-done((bf16[8,256,128]{2,1,0:T(8,128)(2,1)S(1)}, bf16[8,256,128]{2,1,0:T(8,128)(2,1)}, u32[]{:S(2)}, u32[]{:S(2)}) %collective-permute-start.1) | collective-permute-done | bytes 524320 | tf_op jit(solution)/shard_map/ppermute | solution.py:142
  17.6 0.4 collective-permute-start.3
  18.0 0.8 scatter_custom_fusion
  18.8 0.7 all_to_all.9
  19.5 6.6 %all-to-all-start = ((s32[16,1,8]{2,1,0:T(1,128)}), s32[16,1,8]{2,1,0:T(1,128)S(1)}, u32[]{:S(2)}, u32[]{:S(2)}) async-start(s32[16,1,8]{2,1,0:T(1,128)} %bitcast.25), calls=%async_computation | async-start | bytes 16384 | tf_op jit(solution)/shard_map/all_to_all | solution.py:230
  26.1 1.7 collective-permute-start.4
  27.9 11.0 %collective-permute-done.3.refs_5_ = bf16[8,256,128]{2,1,0:T(8,128)(2,1)S(1)} collective-permute-done((bf16[8,256,128]{2,1,0:T(8,128)(2,1)}, bf16[8,256,128]{2,1,0:T(8,128)(2,1)S(1)}, u32[]{:S(2)}, u32[]{:S(2)}) %collective-permute-start.3) | collective-permute-done | bytes 524320 | tf_op jit(solution)/shard_map/ppermute | solution.py:142
  38.9 10.4 %select_bitcast_fusion = (bf16[128,128,128,1]{0,2,1,3:T(8,128)(2,1)}, bf16[128,128,128,1]{0,2,1,3:T(8,128)(2,1)}) fusion(pred[128,128]{1,0:T(8,128)(4,1)S(1)} %get-tuple-element.19, pred[128,128]{1,0:T(8,128)(4,1)S(1)} %get-tuple-element.20, bf16[128,128]{1,0:T(8,128)(2,1)S(1)} %copy-done.11, s32[128,128]{1,0:T(8,128)S(1)} %add_select_fusion), kind=kOutput, calls=%fused_computation.5 | convolution fusion | flops 545259520 | bytes 8519680 | tf_op jit(solution)/shard_map/gk,kij->gij/dot_general | solution.py:189
  49.3 1.4 fusion.1
  50.7 1.3 copy.27
  52.0 6.8 %copy.40 = bf16[128,128,128,1]{2,1,3,0:T(8,128)(2,1)} copy(bf16[128,128,128,1]{0,2,1,3:T(8,128)(2,1)} %get-tuple-element.18) | data formatting | bytes 8388608 | tf_op jit(solution)/shard_map/jit(_where)/select_n | solution.py:193
  58.8 1.1 convert_element_type.74
  60.0 1.3 collective-permute-start.10
  61.3 6.6 %all-to-all-start.1 = ((bf16[16,8,4096]{2,1,0:T(8,128)(2,1)}), bf16[16,8,4096]{2,1,0:T(8,128)(2,1)}, u32[]{:S(2)}, u32[]{:S(2)}) async-start(bf16[16,8,4096]{2,1,0:T(8,128)(2,1)} %fusion.1), calls=%async_computation.1 | async-start | bytes 2097152 | tf_op jit(solution)/shard_map/all_to_all | solution.py:236
  67.9 1.3 collective-permute-start.9
  69.2 2.1 %collective-permute-start.6 = (bf16[8,256,128]{2,1,0:T(8,128)(2,1)}, bf16[8,256,128]{2,1,0:T(8,128)(2,1)}, u32[]{:S(2)}, u32[]{:S(2)}) collective-permute-start(bf16[8,256,128]{2,1,0:T(8,128)(2,1)} %collective-permute-done.4.refs_6_), channel_id=1, source_target_pairs={{0,112},{16,0},{32,16},{48,32},{64,48},{80,64},{96,80},{112,96},{1... | collective-permute-start | bytes 1572872 | tf_op jit(solution)/shard_map/ppermute | solution.py:144
  71.3 1.2 collective-permute-start.7
  72.5 6.2 %fusion.10 = f32[128,2,16,128]{3,2,1,0:T(8,128)} fusion(bf16[128,128,128,1]{2,1,3,0:T(8,128)(2,1)} %copy.40, bf16[2,128,128,16]{1,0,3,2:T(2,128)(2,1)} %convert_element_type.74), kind=kOutput, calls=%fused_computation.21 | convolution fusion | flops 134217728 | bytes 7340032 | tf_op jit(solution)/shard_map/gij,bjgc->bigc/dot_general | solution.py:195
  78.8 6.7 %copy.41 = bf16[128,128,128,1]{2,1,3,0:T(8,128)(2,1)} copy(bf16[128,128,128,1]{0,2,1,3:T(8,128)(2,1)} %get-tuple-element.17) | data formatting | bytes 8388608 | tf_op jit(solution)/shard_map/jit(_where)/select_n | solution.py:194
  85.6 2.3 %pad_maximum_fusion = bf16[256,2048]{1,0:T(8,128)(2,1)} fusion(bf16[256,2048]{1,0:T(8,128)(2,1)} %bitcast.71, bf16[128,2048]{1,0:T(8,128)(2,1)} %collective-permute-done), kind=kLoop, calls=%fused_computation.19 | loop fusion | flops 2097152 | bytes 2621440 | tf_op jit(solution)/shard_map/concatenate | solution.py:182
  87.9 2.3 %copy.30 = bf16[256,2048]{0,1:T(8,128)(2,1)} copy(bf16[256,2048]{1,0:T(8,128)(2,1)} %pad_maximum_fusion) | data formatting | bytes 2097152 | tf_op jit(solution)/shard_map/slice | solution.py:197
  90.2 2.2 %slice.23 = bf16[2,128,128,16]{1,0,3,2:T(2,128)(2,1)} reshape(bf16[256,2048]{0,1:T(8,128)(2,1)} %copy.30) | data formatting | bytes 2097152 | tf_op jit(solution)/shard_map/slice | solution.py:197
  92.3 1.3 collective-permute-start.11
  93.6 1.3 collective-permute-start.12
  94.9 2.3 %collective-permute-done.9.refs_6_ = bf16[8,256,128]{2,1,0:T(8,128)(2,1)S(1)} collective-permute-done((bf16[8,256,128]{2,1,0:T(8,128)(2,1)}, bf16[8,256,128]{2,1,0:T(8,128)(2,1)S(1)}, u32[]{:S(2)}, u32[]{:S(2)}) %collective-permute-start.9) | collective-permute-done | bytes 524320 | tf_op jit(solution)/shard_map/ppermute | solution.py:161
  97.2 1.3 collective-permute-start.13
  98.5 1.3 collective-permute-start.14
  99.8 1.5 collective-permute-start.15
  101.3 5.5 %add_bitcast_fusion = f32[2,128,128,16]{1,3,0,2:T(8,128)S(1)} fusion(f32[128,2,16,128]{3,2,1,0:T(8,128)} %fusion.10, bf16[128,128,128,1]{2,1,3,0:T(8,128)(2,1)} %copy.41, bf16[2,128,128,16]{1,0,3,2:T(2,128)(2,1)} %slice.23), kind=kOutput, calls=%fused_computation.14 | convolution fusion | flops 134742016 | bytes 9437184 | tf_op jit(solution)/shard_map/gij,bjgc->bigc/dot_general | solution.py:196
  106.8 1.1 copy.33
  107.9 1.4 copy.52
  109.3 2.9 %copy.34 = f32[256,2048]{1,0:T(8,128)} copy(f32[256,2048]{0,1:T(8,128)} %bitcast.73) | data formatting | bytes 4194304 | tf_op jit(solution)/shard_map/reshape | solution.py:199
  112.2 1.9 %fusion.12 = f32[256,2048]{1,0:T(8,128)S(1)} fusion(bf16[128,4096]{1,0:T(8,128)(2,1)} %bitcast.28, s32[128]{0:T(128)S(1)} %sub.71), kind=kOutput, calls=%fused_computation.24 | convolution fusion | flops 136085504 | bytes 3146240 | tf_op jit(solution)/shard_map/dot_general | solution.py:243
  114.1 27.5 %shard_map.100 = (f32[4,1,1024]{2,1,0:T(1,128)S(1)}, f32[4,1,1024]{2,1,0:T(1,128)S(1)}, f32[4,128,1024]{2,1,0:T(8,128)}) custom-call(s32[8]{0:T(128)S(1)} %stack.57.refs_0_, bf16[256,2048]{1,0:T(8,128)(2,1)S(1)} %bitcast.68, bf16[8,256,128]{2,1,0:T(8,128)(2,1)S(1)} %maximum_bitcast_fusion.refs_2_, bf16[8,256,128]{2,1,0:T(8,128)(2,1)} %collective-permute-done.1.refs_3_, ...), custom_call_target="tpu_custom_call" | custom-call | tf_op jit(solution)/shard_map/pallas_call | solution.py:117
  141.6 17.5 %shard_map.101 = (f32[4,1,1024]{2,1,0:T(1,128)S(1)}, f32[4,1,1024]{2,1,0:T(1,128)S(1)}, f32[4,128,1024]{2,1,0:T(8,128)S(1)}) custom-call(s32[5]{0:T(128)S(1)} %stack.48.refs_0_, bf16[256,2048]{1,0:T(8,128)(2,1)S(1)} %bitcast.69, f32[4,1,1024]{2,1,0:T(1,128)S(1)} %get-tuple-element.11.refs_2_, f32[4,1,1024]{2,1,0:T(1,128)S(1)} %get-tuple-element.12.refs_3_, ...), custom_call_target="tpu_custom_call" | custom-call | tf_op jit(solution)/shard_map/pallas_call | solution.py:117
  159.2 1.3 copy-done.2
  160.5 12.2 %shard_map.102 = f32[256,2048]{1,0:T(8,128)S(1)} custom-call(s32[3]{0:T(128)S(1)} %stack.47.refs_0_, bf16[256,2048]{1,0:T(8,128)(2,1)S(1)} %bitcast.70, f32[4,1,1024]{2,1,0:T(1,128)S(1)} %get-tuple-element.14.refs_2_, f32[4,1,1024]{2,1,0:T(1,128)S(1)} %get-tuple-element.15.refs_3_, f32[4,128,1024]{2,1,0:T(8,128)} %copy-done.2, ...), custom_call_target="tpu_custom_call" | custom-call | tf_op jit(solution)/shard_map/pallas_call | solution.py:117
  172.8 1.7 fusion.8
  (53 shorter events, 0.5 us)
Async XLA Ops:
  0.0 49.3 %copy-start = (bf16[1,32,4096]{2,1,0:T(8,128)(2,1)S(1)}, bf16[1,32,4096]{2,1,0:T(8,128)(2,1)}, u32[]{:S(2)}) copy-start(bf16[1,32,4096]{2,1,0:T(8,128)(2,1)} %param.17) | copy-start | bytes 786436
  2.6 7.6 %copy-start.12 = (s32[1,32,1]{1,2,0:T(1,128)S(1)}, s32[1,32,1]{1,2,0:T(1,128)}, u32[]{:S(2)}) copy-start(s32[1,32,1]{1,2,0:T(1,128)} %param.18) | copy-start | bytes 388
  2.6 36.3 %copy-start.11 = (bf16[128,128]{1,0:T(8,128)(2,1)S(1)}, bf16[128,128]{1,0:T(8,128)(2,1)}, u32[]{:S(2)}) copy-start(bf16[128,128]{1,0:T(8,128)(2,1)} %param.16) | copy-start | bytes 98308
  2.7 15.0 %collective-permute-start.1 = (bf16[8,256,128]{2,1,0:T(8,128)(2,1)S(1)}, bf16[8,256,128]{2,1,0:T(8,128)(2,1)}, u32[]{:S(2)}, u32[]{:S(2)}) collective-permute-start(bf16[8,256,128]{2,1,0:T(8,128)(2,1)S(1)} %maximum_bitcast_fusion.refs_2_), channel_id=1, source_target_pairs={{0,16},{16,32},{32,48},{48,64},{64,80},{80,96},{96,112},{112,0},{1... | collective-permute-start | bytes 1572872 | tf_op jit(solution)/shard_map/ppermute | solution.py:142
  2.8 23.4 %collective-permute-start.2 = (bf16[8,256,128]{2,1,0:T(8,128)(2,1)S(1)}, bf16[8,256,128]{2,1,0:T(8,128)(2,1)S(1)}, u32[]{:S(2)}, u32[]{:S(2)}) collective-permute-start(bf16[8,256,128]{2,1,0:T(8,128)(2,1)S(1)} %maximum_bitcast_fusion.refs_2_), channel_id=1, source_target_pairs={{0,112},{16,0},{32,16},{48,32},{64,48},{80,64},{96,80},{112,96},{1... | collective-permute-start | bytes 1572872 | tf_op jit(solution)/shard_map/ppermute | solution.py:144
  4.8 87.6 %collective-permute-start.8 = (bf16[8,256,128]{2,1,0:T(8,128)(2,1)S(1)}, bf16[8,256,128]{2,1,0:T(8,128)(2,1)S(1)}, u32[]{:S(2)}, u32[]{:S(2)}) collective-permute-start(bf16[8,256,128]{2,1,0:T(8,128)(2,1)S(1)} %maximum_bitcast_fusion.refs_2_), channel_id=1, source_target_pairs={{0,128},{16,144},{32,160},{48,176},{64,192},{80,208},{96,224},{112... | collective-permute-start | bytes 1572872 | tf_op jit(solution)/shard_map/ppermute | solution.py:161
  8.0 42.7 %copy-start.7 = (bf16[1,256,2048]{2,1,0:T(8,128)(2,1)}, bf16[1,256,2048]{2,1,0:T(8,128)(2,1)S(1)}, u32[]{:S(2)}) copy-start(bf16[1,256,2048]{2,1,0:T(8,128)(2,1)S(1)} %multiply_convert_fusion) | copy-start | bytes 3145732
  8.9 58.9 %collective-permute-start = (bf16[128,2048]{1,0:T(8,128)(2,1)}, bf16[128,2048]{1,0:T(8,128)(2,1)}, u32[]{:S(2)}, u32[]{:S(2)}) collective-permute-start(bf16[128,2048]{1,0:T(8,128)(2,1)} %slice_bitcast_fusion), channel_id=1, source_target_pairs={{0,16},{16,32},{32,48},{48,64},{64,80},{80,96},{96,112},{112,128},... | collective-permute-start | bytes 1572872 | tf_op jit(solution)/shard_map/ppermute | solution.py:21
  17.6 21.2 %collective-permute-start.3 = (bf16[8,256,128]{2,1,0:T(8,128)(2,1)}, bf16[8,256,128]{2,1,0:T(8,128)(2,1)S(1)}, u32[]{:S(2)}, u32[]{:S(2)}) collective-permute-start(bf16[8,256,128]{2,1,0:T(8,128)(2,1)} %collective-permute-done.1.refs_3_), channel_id=1, source_target_pairs={{0,16},{16,32},{32,48},{48,64},{64,80},{80,96},{96,112},{112,0},{1... | collective-permute-start | bytes 1572872 | tf_op jit(solution)/shard_map/ppermute | solution.py:142
  19.5 41.7 %all-to-all-start = ((s32[16,1,8]{2,1,0:T(1,128)}), s32[16,1,8]{2,1,0:T(1,128)S(1)}, u32[]{:S(2)}, u32[]{:S(2)}) async-start(s32[16,1,8]{2,1,0:T(1,128)} %bitcast.25), calls=%async_computation | async-start | bytes 16384 | tf_op jit(solution)/shard_map/all_to_all | solution.py:230
  26.1 33.8 %copy-start.3 = (bf16[8,256,128]{2,1,0:T(8,128)(2,1)}, bf16[8,256,128]{2,1,0:T(8,128)(2,1)S(1)}, u32[]{:S(2)}) copy-start(bf16[8,256,128]{2,1,0:T(8,128)(2,1)S(1)} %collective-permute-done.2.refs_4_) | copy-start | bytes 1572868
  26.1 43.0 %collective-permute-start.4 = (bf16[8,256,128]{2,1,0:T(8,128)(2,1)S(1)}, bf16[8,256,128]{2,1,0:T(8,128)(2,1)}, u32[]{:S(2)}, u32[]{:S(2)}) collective-permute-start(bf16[8,256,128]{2,1,0:T(8,128)(2,1)S(1)} %collective-permute-done.2.refs_4_), channel_id=1, source_target_pairs={{0,112},{16,0},{32,16},{48,32},{64,48},{80,64},{96,80},{112,96},{1... | collective-permute-start | bytes 1572872 | tf_op jit(solution)/shard_map/ppermute | solution.py:144
  38.9 10.4 %copy-start.5 = (bf16[8,256,128]{2,1,0:T(8,128)(2,1)}, bf16[8,256,128]{2,1,0:T(8,128)(2,1)S(1)}, u32[]{:S(2)}) copy-start(bf16[8,256,128]{2,1,0:T(8,128)(2,1)S(1)} %collective-permute-done.3.refs_5_) | copy-start | bytes 1572868
  38.9 32.4 %collective-permute-start.5 = (bf16[8,256,128]{2,1,0:T(8,128)(2,1)S(1)}, bf16[8,256,128]{2,1,0:T(8,128)(2,1)}, u32[]{:S(2)}, u32[]{:S(2)}) collective-permute-start(bf16[8,256,128]{2,1,0:T(8,128)(2,1)S(1)} %collective-permute-done.3.refs_5_), channel_id=1, source_target_pairs={{0,16},{16,32},{32,48},{48,64},{64,80},{80,96},{96,112},{112,0},{1... | collective-permute-start | bytes 1572872 | tf_op jit(solution)/shard_map/ppermute | solution.py:142
  52.0 6.8 %copy-start.9 = (bf16[1,256,2048]{1,2,0:T(8,128)(2,1)S(1)}, bf16[1,256,2048]{1,2,0:T(8,128)(2,1)}, u32[]{:S(2)}) copy-start(bf16[1,256,2048]{1,2,0:T(8,128)(2,1)} %copy.27) | copy-start | bytes 3145732
  60.0 33.7 %collective-permute-start.10 = (bf16[8,256,128]{2,1,0:T(8,128)(2,1)S(1)}, bf16[8,256,128]{2,1,0:T(8,128)(2,1)S(1)}, u32[]{:S(2)}, u32[]{:S(2)}) collective-permute-start(bf16[8,256,128]{2,1,0:T(8,128)(2,1)S(1)} %collective-permute-done.2.refs_4_), channel_id=1, source_target_pairs={{0,128},{16,144},{32,160},{48,176},{64,192},{80,208},{96,224},{112... | collective-permute-start | bytes 1572872 | tf_op jit(solution)/shard_map/ppermute | solution.py:161
  61.3 51.0 %all-to-all-start.1 = ((bf16[16,8,4096]{2,1,0:T(8,128)(2,1)}), bf16[16,8,4096]{2,1,0:T(8,128)(2,1)}, u32[]{:S(2)}, u32[]{:S(2)}) async-start(bf16[16,8,4096]{2,1,0:T(8,128)(2,1)} %fusion.1), calls=%async_computation.1 | async-start | bytes 2097152 | tf_op jit(solution)/shard_map/all_to_all | solution.py:236
  67.9 29.4 %collective-permute-start.9 = (bf16[8,256,128]{2,1,0:T(8,128)(2,1)}, bf16[8,256,128]{2,1,0:T(8,128)(2,1)S(1)}, u32[]{:S(2)}, u32[]{:S(2)}) collective-permute-start(bf16[8,256,128]{2,1,0:T(8,128)(2,1)} %collective-permute-done.1.refs_3_), channel_id=1, source_target_pairs={{0,128},{16,144},{32,160},{48,176},{64,192},{80,208},{96,224},{112... | collective-permute-start | bytes 1572872 | tf_op jit(solution)/shard_map/ppermute | solution.py:161
  69.2 29.4 %collective-permute-start.6 = (bf16[8,256,128]{2,1,0:T(8,128)(2,1)}, bf16[8,256,128]{2,1,0:T(8,128)(2,1)}, u32[]{:S(2)}, u32[]{:S(2)}) collective-permute-start(bf16[8,256,128]{2,1,0:T(8,128)(2,1)} %collective-permute-done.4.refs_6_), channel_id=1, source_target_pairs={{0,112},{16,0},{32,16},{48,32},{64,48},{80,64},{96,80},{112,96},{1... | collective-permute-start | bytes 1572872 | tf_op jit(solution)/shard_map/ppermute | solution.py:144
  71.3 28.6 %collective-permute-start.7 = (bf16[8,256,128]{2,1,0:T(8,128)(2,1)}, bf16[8,256,128]{2,1,0:T(8,128)(2,1)}, u32[]{:S(2)}, u32[]{:S(2)}) collective-permute-start(bf16[8,256,128]{2,1,0:T(8,128)(2,1)} %collective-permute-done.5.refs_7_), channel_id=1, source_target_pairs={{0,16},{16,32},{32,48},{48,64},{64,80},{80,96},{96,112},{112,0},{1... | collective-permute-start | bytes 1572872 | tf_op jit(solution)/shard_map/ppermute | solution.py:142
  92.3 49.2 %collective-permute-start.11 = (bf16[8,256,128]{2,1,0:T(8,128)(2,1)}, bf16[8,256,128]{2,1,0:T(8,128)(2,1)S(1)}, u32[]{:S(2)}, u32[]{:S(2)}) collective-permute-start(bf16[8,256,128]{2,1,0:T(8,128)(2,1)} %copy-done.5), channel_id=1, source_target_pairs={{0,128},{16,144},{32,160},{48,176},{64,192},{80,208},{96,224},{112... | collective-permute-start | bytes 1572872 | tf_op jit(solution)/shard_map/ppermute | solution.py:161
  93.6 47.9 %collective-permute-start.12 = (bf16[8,256,128]{2,1,0:T(8,128)(2,1)}, bf16[8,256,128]{2,1,0:T(8,128)(2,1)S(1)}, u32[]{:S(2)}, u32[]{:S(2)}) collective-permute-start(bf16[8,256,128]{2,1,0:T(8,128)(2,1)} %collective-permute-done.4.refs_6_), channel_id=1, source_target_pairs={{0,128},{16,144},{32,160},{48,176},{64,192},{80,208},{96,224},{112... | collective-permute-start | bytes 1572872 | tf_op jit(solution)/shard_map/ppermute | solution.py:161
  97.2 63.2 %collective-permute-start.13 = (bf16[8,256,128]{2,1,0:T(8,128)(2,1)}, bf16[8,256,128]{2,1,0:T(8,128)(2,1)}, u32[]{:S(2)}, u32[]{:S(2)}) collective-permute-start(bf16[8,256,128]{2,1,0:T(8,128)(2,1)} %collective-permute-done.5.refs_7_), channel_id=1, source_target_pairs={{0,128},{16,144},{32,160},{48,176},{64,192},{80,208},{96,224},{112... | collective-permute-start | bytes 1572872 | tf_op jit(solution)/shard_map/ppermute | solution.py:161
  98.5 61.9 %collective-permute-start.14 = (bf16[8,256,128]{2,1,0:T(8,128)(2,1)}, bf16[8,256,128]{2,1,0:T(8,128)(2,1)}, u32[]{:S(2)}, u32[]{:S(2)}) collective-permute-start(bf16[8,256,128]{2,1,0:T(8,128)(2,1)} %collective-permute-done.6.refs_8_), channel_id=1, source_target_pairs={{0,128},{16,144},{32,160},{48,176},{64,192},{80,208},{96,224},{112... | collective-permute-start | bytes 1572872 | tf_op jit(solution)/shard_map/ppermute | solution.py:161
  99.8 60.6 %collective-permute-start.15 = (bf16[8,256,128]{2,1,0:T(8,128)(2,1)}, bf16[8,256,128]{2,1,0:T(8,128)(2,1)}, u32[]{:S(2)}, u32[]{:S(2)}) collective-permute-start(bf16[8,256,128]{2,1,0:T(8,128)(2,1)} %collective-permute-done.7.refs_9_), channel_id=1, source_target_pairs={{0,128},{16,144},{32,160},{48,176},{64,192},{80,208},{96,224},{112... | collective-permute-start | bytes 1572872 | tf_op jit(solution)/shard_map/ppermute | solution.py:161
  112.2 1.9 %copy-start.1 = (bf16[1,256,2048]{2,1,0:T(8,128)(2,1)S(1)}, bf16[1,256,2048]{2,1,0:T(8,128)(2,1)}, u32[]{:S(2)}) copy-start(bf16[1,256,2048]{2,1,0:T(8,128)(2,1)} %param.10) | copy-start | bytes 3145732
  112.2 1.9 %copy-start.4 = (bf16[8,256,128]{2,1,0:T(8,128)(2,1)S(1)}, bf16[8,256,128]{2,1,0:T(8,128)(2,1)}, u32[]{:S(2)}) copy-start(bf16[8,256,128]{2,1,0:T(8,128)(2,1)} %copy-done.3) | copy-start | bytes 1572868
  112.2 1.9 %copy-start.6 = (bf16[8,256,128]{2,1,0:T(8,128)(2,1)S(1)}, bf16[8,256,128]{2,1,0:T(8,128)(2,1)}, u32[]{:S(2)}) copy-start(bf16[8,256,128]{2,1,0:T(8,128)(2,1)} %copy-done.5) | copy-start | bytes 1572868
  159.2 1.3 copy-start.2
  160.5 12.3 %copy-start.8 = (f32[256,2048]{1,0:T(8,128)S(1)}, f32[256,2048]{1,0:T(8,128)}, u32[]{:S(2)}) copy-start(f32[256,2048]{1,0:T(8,128)} %copy.34) | copy-start | bytes 6291460
  160.5 12.3 %copy-start.10 = (bf16[1,256,2048]{2,1,0:T(8,128)(2,1)S(1)}, bf16[1,256,2048]{2,1,0:T(8,128)(2,1)}, u32[]{:S(2)}) copy-start(bf16[1,256,2048]{2,1,0:T(8,128)(2,1)} %param.14) | copy-start | bytes 3145732
where the time goes:
time: 175 us; the launch traced here: 174 us
  Pallas kernels  57.2 us (33%)
  starting transfers between devices  32.4 us (19%)
  local copies, waits for them, and re-layouts  32.3 us (18%)
  matrix products  25.4 us (15%)
  waiting for transfers between devices  20.6 us (12%)
  other arithmetic  6.08 us (3%)
    pallas_call x3, Pallas kernels, flash(): pl.pallas_call(kernel, out_shape=out_shape, in_specs=[pl.BlockSpec(memory...  57.2 us
    ppermute x4, waiting for transfers between devices, attention(): lefts.append(lax.ppermute(lefts[-1], 'ctx', plus))  18.3 us
    ppermute x8, starting transfers between devices, attention(): blocks.append(lax.ppermute(piece, 'ctx', up))  10.5 us
    dot_general x1, matrix products, conv_body(): jnp.einsum('gk,kij->gij', filters, selector, preferred_element_type=jnp.f...  10.4 us
    select_n x1, local copies, waits for them, and re-layouts, conv_body(): lower = jnp.where((lag >= 0)[None], circulant, nothing)  6.78 us
    select_n x1, local copies, waits for them, and re-layouts, conv_body(): upper = jnp.where((lag < 0)[None], circulant, nothing)  6.7 us
    all_to_all x1, starting transfers between devices, route_hints(): lax.all_to_all(buffer.reshape(dp_count, cap, entries), 'dp', split_axis=0...  6.59 us
    all_to_all x1, starting transfers between devices, route_hints(): lax.all_to_all(row_buffer.reshape(dp_count, cap), 'dp', split_axis=0, con...  6.58 us
  transfers between devices with their start and end apart: 18, of which 3 were waited for; matrix products, arithmetic and copies ran while one was open for 33% of the time, Pallas kernels for 26%

commit v1 on v0

--- a/solution.py
+++ b/solution.py
@@ -41,7 +41,7 @@
     for g in range(KV_HEADS):
         for j in range(grp):
             col = (g * grp + j) * HEAD_DIM
-            qs_sc[g, j * tok : (j + 1) * tok, :] = q_ref[:, col : col + HEAD_DIM]
+            qs_sc[g, :, j * tok : (j + 1) * tok] = q_ref[:, col : col + HEAD_DIM].T
     if first:
         m_sc[...] = jnp.full_like(m_sc, NEG)
         l_sc[...] = jnp.zeros_like(l_sc)
@@ -55,9 +55,7 @@
         def one(g, carry):
             k = kv_ref[g]
             v = kv_ref[KV_HEADS + g]
-            s = lax.dot_general(
-                k, qs_sc[g], (((1,), (1,)), ((), ())), preferred_element_type=jnp.float32
-            ) * scale
+            s = jnp.dot(k, qs_sc[g], preferred_element_type=jnp.float32) * scale
             if masked:
                 rows = lax.broadcasted_iota(jnp.int32, s.shape, 0)
                 cols = lax.broadcasted_iota(jnp.int32, s.shape, 1) % tok
@@ -121,7 +119,7 @@
         + [vmem] * (1 + len(extra) + len(blocks)),
         out_specs=out_specs,
         scratch_shapes=[
-            pltpu.VMEM((KV_HEADS, grp * tok, HEAD_DIM), jnp.bfloat16),
+            pltpu.VMEM((KV_HEADS, HEAD_DIM, grp * tok), jnp.bfloat16),
             pltpu.VMEM((KV_HEADS, 1, grp * tok), jnp.float32),
             pltpu.VMEM((KV_HEADS, 1, grp * tok), jnp.float32),
             pltpu.VMEM((KV_HEADS, HEAD_DIM, grp * tok), jnp.float32),

time: 175 us -> 175 us (level)
  no operation moved by 1% of the time
where the time goes in v1:
time: 175 us; the launch traced here: 174 us
  Pallas kernels  56.6 us (32%)
  starting transfers between devices  32.4 us (19%)
  local copies, waits for them, and re-layouts  32.3 us (18%)
  matrix products  25.4 us (15%)
  waiting for transfers between devices  20.6 us (12%)
  other arithmetic  6.08 us (3%)
    pallas_call x3, Pallas kernels, flash(): pl.pallas_call(kernel, out_shape=out_shape, in_specs=[pl.BlockSpec(memory...  56.6 us
    ppermute x4, waiting for transfers between devices, attention(): lefts.append(lax.ppermute(lefts[-1], 'ctx', plus))  18.3 us
    ppermute x8, starting transfers between devices, attention(): blocks.append(lax.ppermute(piece, 'ctx', up))  10.5 us
    dot_general x1, matrix products, conv_body(): jnp.einsum('gk,kij->gij', filters, selector, preferred_element_type=jnp.f...  10.4 us
    select_n x1, local copies, waits for them, and re-layouts, conv_body(): lower = jnp.where((lag >= 0)[None], circulant, nothing)  6.78 us
    select_n x1, local copies, waits for them, and re-layouts, conv_body(): upper = jnp.where((lag < 0)[None], circulant, nothing)  6.7 us
    all_to_all x1, starting transfers between devices, route_hints(): lax.all_to_all(buffer.reshape(dp_count, cap, entries), 'dp', split_axis=0...  6.59 us
    all_to_all x1, starting transfers between devices, route_hints(): lax.all_to_all(row_buffer.reshape(dp_count, cap), 'dp', split_axis=0, con...  6.58 us
  transfers between devices with their start and end apart: 18, of which 3 were waited for; matrix products, arithmetic and copies ran while one was open for 33% of the time, Pallas kernels for 26%

profile of v1, /device:TPU:234, one launch (start us, length us, event | category | flops | bytes accessed | tf_op | source)
XLA Modules:
  0.0 173.9 jit_solution(13384458000409557811)
XLA Ops:
  0.0 1.1 copy.35
  1.1 0.2 copy.37
  1.3 1.1 copy.36
  2.4 0.2 copy.38
  2.8 2.0 %collective-permute-start.2 = (bf16[8,256,128]{2,1,0:T(8,128)(2,1)S(1)}, bf16[8,256,128]{2,1,0:T(8,128)(2,1)S(1)}, u32[]{:S(2)}, u32[]{:S(2)}) collective-permute-start(bf16[8,256,128]{2,1,0:T(8,128)(2,1)S(1)} %maximum_bitcast_fusion.refs_2_), channel_id=1, source_target_pairs={{0,112},{16,0},{32,16},{48,32},{64,48},{80,64},{96,80},{112,96},{1... | collective-permute-start | bytes 1572872 | tf_op jit(solution)/shard_map/ppermute | solution.py:142
  4.8 1.3 collective-permute-start.8
  6.1 1.9 %multiply_convert_fusion = bf16[1,256,2048]{2,1,0:T(8,128)(2,1)S(1)} fusion(bf16[1,256,2048]{2,1,0:T(8,128)(2,1)} %param.15, bf16[1,256,2048]{2,1,0:T(8,128)(2,1)} %param.13), kind=kLoop, calls=%fused_computation.15 | loop fusion | flops 2097152 | bytes 3145728 | tf_op jit(solution)/shard_map/convert_element_type | solution.py:174
  8.0 0.9 slice_bitcast_fusion
  8.9 1.3 collective-permute-start
  10.2 0.1 fusion.7
  10.4 7.3 %collective-permute-done.1.refs_3_ = bf16[8,256,128]{2,1,0:T(8,128)(2,1)} collective-permute-done((bf16[8,256,128]{2,1,0:T(8,128)(2,1)S(1)}, bf16[8,256,128]{2,1,0:T(8,128)(2,1)}, u32[]{:S(2)}, u32[]{:S(2)}) %collective-permute-start.1) | collective-permute-done | bytes 524320 | tf_op jit(solution)/shard_map/ppermute | solution.py:140
  17.6 0.4 collective-permute-start.3
  18.0 0.8 scatter_custom_fusion
  18.8 0.7 all_to_all.9
  19.5 6.6 %all-to-all-start = ((s32[16,1,8]{2,1,0:T(1,128)}), s32[16,1,8]{2,1,0:T(1,128)S(1)}, u32[]{:S(2)}, u32[]{:S(2)}) async-start(s32[16,1,8]{2,1,0:T(1,128)} %bitcast.25), calls=%async_computation | async-start | bytes 16384 | tf_op jit(solution)/shard_map/all_to_all | solution.py:228
  26.1 1.7 collective-permute-start.4
  27.9 11.0 %collective-permute-done.3.refs_5_ = bf16[8,256,128]{2,1,0:T(8,128)(2,1)S(1)} collective-permute-done((bf16[8,256,128]{2,1,0:T(8,128)(2,1)}, bf16[8,256,128]{2,1,0:T(8,128)(2,1)S(1)}, u32[]{:S(2)}, u32[]{:S(2)}) %collective-permute-start.3) | collective-permute-done | bytes 524320 | tf_op jit(solution)/shard_map/ppermute | solution.py:140
  38.9 10.4 %select_bitcast_fusion = (bf16[128,128,128,1]{0,2,1,3:T(8,128)(2,1)}, bf16[128,128,128,1]{0,2,1,3:T(8,128)(2,1)}) fusion(pred[128,128]{1,0:T(8,128)(4,1)S(1)} %get-tuple-element.19, pred[128,128]{1,0:T(8,128)(4,1)S(1)} %get-tuple-element.20, bf16[128,128]{1,0:T(8,128)(2,1)S(1)} %copy-done.11, s32[128,128]{1,0:T(8,128)S(1)} %add_select_fusion), kind=kOutput, calls=%fused_computation.5 | convolution fusion | flops 545259520 | bytes 8519680 | tf_op jit(solution)/shard_map/gk,kij->gij/dot_general | solution.py:187
  49.3 1.4 fusion.1
  50.7 1.3 copy.27
  52.0 6.8 %copy.40 = bf16[128,128,128,1]{2,1,3,0:T(8,128)(2,1)} copy(bf16[128,128,128,1]{0,2,1,3:T(8,128)(2,1)} %get-tuple-element.18) | data formatting | bytes 8388608 | tf_op jit(solution)/shard_map/jit(_where)/select_n | solution.py:191
  58.8 1.1 convert_element_type.74
  60.0 1.3 collective-permute-start.10
  61.3 6.6 %all-to-all-start.1 = ((bf16[16,8,4096]{2,1,0:T(8,128)(2,1)}), bf16[16,8,4096]{2,1,0:T(8,128)(2,1)}, u32[]{:S(2)}, u32[]{:S(2)}) async-start(bf16[16,8,4096]{2,1,0:T(8,128)(2,1)} %fusion.1), calls=%async_computation.1 | async-start | bytes 2097152 | tf_op jit(solution)/shard_map/all_to_all | solution.py:234
  67.9 1.3 collective-permute-start.9
  69.2 2.1 %collective-permute-start.6 = (bf16[8,256,128]{2,1,0:T(8,128)(2,1)}, bf16[8,256,128]{2,1,0:T(8,128)(2,1)}, u32[]{:S(2)}, u32[]{:S(2)}) collective-permute-start(bf16[8,256,128]{2,1,0:T(8,128)(2,1)} %collective-permute-done.4.refs_6_), channel_id=1, source_target_pairs={{0,112},{16,0},{32,16},{48,32},{64,48},{80,64},{96,80},{112,96},{1... | collective-permute-start | bytes 1572872 | tf_op jit(solution)/shard_map/ppermute | solution.py:142
  71.3 1.2 collective-permute-start.7
  72.5 6.2 %fusion.10 = f32[128,2,16,128]{3,2,1,0:T(8,128)} fusion(bf16[128,128,128,1]{2,1,3,0:T(8,128)(2,1)} %copy.40, bf16[2,128,128,16]{1,0,3,2:T(2,128)(2,1)} %convert_element_type.74), kind=kOutput, calls=%fused_computation.21 | convolution fusion | flops 134217728 | bytes 7340032 | tf_op jit(solution)/shard_map/gij,bjgc->bigc/dot_general | solution.py:193
  78.8 6.7 %copy.41 = bf16[128,128,128,1]{2,1,3,0:T(8,128)(2,1)} copy(bf16[128,128,128,1]{0,2,1,3:T(8,128)(2,1)} %get-tuple-element.17) | data formatting | bytes 8388608 | tf_op jit(solution)/shard_map/jit(_where)/select_n | solution.py:192
  85.6 2.3 %pad_maximum_fusion = bf16[256,2048]{1,0:T(8,128)(2,1)} fusion(bf16[256,2048]{1,0:T(8,128)(2,1)} %bitcast.71, bf16[128,2048]{1,0:T(8,128)(2,1)} %collective-permute-done), kind=kLoop, calls=%fused_computation.19 | loop fusion | flops 2097152 | bytes 2621440 | tf_op jit(solution)/shard_map/concatenate | solution.py:180
  87.9 2.3 %copy.30 = bf16[256,2048]{0,1:T(8,128)(2,1)} copy(bf16[256,2048]{1,0:T(8,128)(2,1)} %pad_maximum_fusion) | data formatting | bytes 2097152 | tf_op jit(solution)/shard_map/slice | solution.py:195
  90.2 2.2 %slice.23 = bf16[2,128,128,16]{1,0,3,2:T(2,128)(2,1)} reshape(bf16[256,2048]{0,1:T(8,128)(2,1)} %copy.30) | data formatting | bytes 2097152 | tf_op jit(solution)/shard_map/slice | solution.py:195
  92.3 1.3 collective-permute-start.11
  93.6 1.3 collective-permute-start.12
  94.9 2.3 %collective-permute-done.9.refs_6_ = bf16[8,256,128]{2,1,0:T(8,128)(2,1)S(1)} collective-permute-done((bf16[8,256,128]{2,1,0:T(8,128)(2,1)}, bf16[8,256,128]{2,1,0:T(8,128)(2,1)S(1)}, u32[]{:S(2)}, u32[]{:S(2)}) %collective-permute-start.9) | collective-permute-done | bytes 524320 | tf_op jit(solution)/shard_map/ppermute | solution.py:159
  97.2 1.3 collective-permute-start.13
  98.5 1.3 collective-permute-start.14
  99.8 1.5 collective-permute-start.15
  101.3 5.5 %add_bitcast_fusion = f32[2,128,128,16]{1,3,0,2:T(8,128)S(1)} fusion(f32[128,2,16,128]{3,2,1,0:T(8,128)} %fusion.10, bf16[128,128,128,1]{2,1,3,0:T(8,128)(2,1)} %copy.41, bf16[2,128,128,16]{1,0,3,2:T(2,128)(2,1)} %slice.23), kind=kOutput, calls=%fused_computation.14 | convolution fusion | flops 134742016 | bytes 9437184 | tf_op jit(solution)/shard_map/gij,bjgc->bigc/dot_general | solution.py:194
  106.8 1.1 copy.33
  107.9 1.4 copy.52
  109.3 2.9 %copy.34 = f32[256,2048]{1,0:T(8,128)} copy(f32[256,2048]{0,1:T(8,128)} %bitcast.73) | data formatting | bytes 4194304 | tf_op jit(solution)/shard_map/reshape | solution.py:197
  112.2 1.9 %fusion.12 = f32[256,2048]{1,0:T(8,128)S(1)} fusion(bf16[128,4096]{1,0:T(8,128)(2,1)} %bitcast.28, s32[128]{0:T(128)S(1)} %sub.71), kind=kOutput, calls=%fused_computation.24 | convolution fusion | flops 136085504 | bytes 3146240 | tf_op jit(solution)/shard_map/dot_general | solution.py:241
  114.1 27.1 %shard_map.100 = (f32[4,1,1024]{2,1,0:T(1,128)S(1)}, f32[4,1,1024]{2,1,0:T(1,128)S(1)}, f32[4,128,1024]{2,1,0:T(8,128)}) custom-call(s32[8]{0:T(128)S(1)} %stack.57.refs_0_, bf16[256,2048]{1,0:T(8,128)(2,1)S(1)} %bitcast.68, bf16[8,256,128]{2,1,0:T(8,128)(2,1)S(1)} %maximum_bitcast_fusion.refs_2_, bf16[8,256,128]{2,1,0:T(8,128)(2,1)} %collective-permute-done.1.refs_3_, ...), custom_call_target="tpu_custom_call" | custom-call | tf_op jit(solution)/shard_map/pallas_call | solution.py:115
  141.3 17.4 %shard_map.101 = (f32[4,1,1024]{2,1,0:T(1,128)S(1)}, f32[4,1,1024]{2,1,0:T(1,128)S(1)}, f32[4,128,1024]{2,1,0:T(8,128)S(1)}) custom-call(s32[5]{0:T(128)S(1)} %stack.48.refs_0_, bf16[256,2048]{1,0:T(8,128)(2,1)S(1)} %bitcast.69, f32[4,1,1024]{2,1,0:T(1,128)S(1)} %get-tuple-element.11.refs_2_, f32[4,1,1024]{2,1,0:T(1,128)S(1)} %get-tuple-element.12.refs_3_, ...), custom_call_target="tpu_custom_call" | custom-call | tf_op jit(solution)/shard_map/pallas_call | solution.py:115
  158.6 1.3 copy-done.2
  160.0 12.2 %shard_map.102 = f32[256,2048]{1,0:T(8,128)S(1)} custom-call(s32[3]{0:T(128)S(1)} %stack.47.refs_0_, bf16[256,2048]{1,0:T(8,128)(2,1)S(1)} %bitcast.70, f32[4,1,1024]{2,1,0:T(1,128)S(1)} %get-tuple-element.14.refs_2_, f32[4,1,1024]{2,1,0:T(1,128)S(1)} %get-tuple-element.15.refs_3_, f32[4,128,1024]{2,1,0:T(8,128)} %copy-done.2, ...), custom_call_target="tpu_custom_call" | custom-call | tf_op jit(solution)/shard_map/pallas_call | solution.py:115
  172.2 1.7 fusion.8
  (53 shorter events, 0.5 us)
Async XLA Ops:
  0.0 49.3 %copy-start = (bf16[1,32,4096]{2,1,0:T(8,128)(2,1)S(1)}, bf16[1,32,4096]{2,1,0:T(8,128)(2,1)}, u32[]{:S(2)}) copy-start(bf16[1,32,4096]{2,1,0:T(8,128)(2,1)} %param.17) | copy-start | bytes 786436
  2.6 7.6 %copy-start.12 = (s32[1,32,1]{1,2,0:T(1,128)S(1)}, s32[1,32,1]{1,2,0:T(1,128)}, u32[]{:S(2)}) copy-start(s32[1,32,1]{1,2,0:T(1,128)} %param.18) | copy-start | bytes 388
  2.6 36.3 %copy-start.11 = (bf16[128,128]{1,0:T(8,128)(2,1)S(1)}, bf16[128,128]{1,0:T(8,128)(2,1)}, u32[]{:S(2)}) copy-start(bf16[128,128]{1,0:T(8,128)(2,1)} %param.16) | copy-start | bytes 98308
  2.7 15.0 %collective-permute-start.1 = (bf16[8,256,128]{2,1,0:T(8,128)(2,1)S(1)}, bf16[8,256,128]{2,1,0:T(8,128)(2,1)}, u32[]{:S(2)}, u32[]{:S(2)}) collective-permute-start(bf16[8,256,128]{2,1,0:T(8,128)(2,1)S(1)} %maximum_bitcast_fusion.refs_2_), channel_id=1, source_target_pairs={{0,16},{16,32},{32,48},{48,64},{64,80},{80,96},{96,112},{112,0},{1... | collective-permute-start | bytes 1572872 | tf_op jit(solution)/shard_map/ppermute | solution.py:140
  2.8 23.4 %collective-permute-start.2 = (bf16[8,256,128]{2,1,0:T(8,128)(2,1)S(1)}, bf16[8,256,128]{2,1,0:T(8,128)(2,1)S(1)}, u32[]{:S(2)}, u32[]{:S(2)}) collective-permute-start(bf16[8,256,128]{2,1,0:T(8,128)(2,1)S(1)} %maximum_bitcast_fusion.refs_2_), channel_id=1, source_target_pairs={{0,112},{16,0},{32,16},{48,32},{64,48},{80,64},{96,80},{112,96},{1... | collective-permute-start | bytes 1572872 | tf_op jit(solution)/shard_map/ppermute | solution.py:142
  4.8 87.6 %collective-permute-start.8 = (bf16[8,256,128]{2,1,0:T(8,128)(2,1)S(1)}, bf16[8,256,128]{2,1,0:T(8,128)(2,1)S(1)}, u32[]{:S(2)}, u32[]{:S(2)}) collective-permute-start(bf16[8,256,128]{2,1,0:T(8,128)(2,1)S(1)} %maximum_bitcast_fusion.refs_2_), channel_id=1, source_target_pairs={{0,128},{16,144},{32,160},{48,176},{64,192},{80,208},{96,224},{112... | collective-permute-start | bytes 1572872 | tf_op jit(solution)/shard_map/ppermute | solution.py:159
  8.0 42.7 %copy-start.7 = (bf16[1,256,2048]{2,1,0:T(8,128)(2,1)}, bf16[1,256,2048]{2,1,0:T(8,128)(2,1)S(1)}, u32[]{:S(2)}) copy-start(bf16[1,256,2048]{2,1,0:T(8,128)(2,1)S(1)} %multiply_convert_fusion) | copy-start | bytes 3145732
  8.9 58.9 %collective-permute-start = (bf16[128,2048]{1,0:T(8,128)(2,1)}, bf16[128,2048]{1,0:T(8,128)(2,1)}, u32[]{:S(2)}, u32[]{:S(2)}) collective-permute-start(bf16[128,2048]{1,0:T(8,128)(2,1)} %slice_bitcast_fusion), channel_id=1, source_target_pairs={{0,16},{16,32},{32,48},{48,64},{64,80},{80,96},{96,112},{112,128},... | collective-permute-start | bytes 1572872 | tf_op jit(solution)/shard_map/ppermute | solution.py:21
  17.6 21.2 %collective-permute-start.3 = (bf16[8,256,128]{2,1,0:T(8,128)(2,1)}, bf16[8,256,128]{2,1,0:T(8,128)(2,1)S(1)}, u32[]{:S(2)}, u32[]{:S(2)}) collective-permute-start(bf16[8,256,128]{2,1,0:T(8,128)(2,1)} %collective-permute-done.1.refs_3_), channel_id=1, source_target_pairs={{0,16},{16,32},{32,48},{48,64},{64,80},{80,96},{96,112},{112,0},{1... | collective-permute-start | bytes 1572872 | tf_op jit(solution)/shard_map/ppermute | solution.py:140
  19.5 41.7 %all-to-all-start = ((s32[16,1,8]{2,1,0:T(1,128)}), s32[16,1,8]{2,1,0:T(1,128)S(1)}, u32[]{:S(2)}, u32[]{:S(2)}) async-start(s32[16,1,8]{2,1,0:T(1,128)} %bitcast.25), calls=%async_computation | async-start | bytes 16384 | tf_op jit(solution)/shard_map/all_to_all | solution.py:228
  26.1 33.8 %copy-start.3 = (bf16[8,256,128]{2,1,0:T(8,128)(2,1)}, bf16[8,256,128]{2,1,0:T(8,128)(2,1)S(1)}, u32[]{:S(2)}) copy-start(bf16[8,256,128]{2,1,0:T(8,128)(2,1)S(1)} %collective-permute-done.2.refs_4_) | copy-start | bytes 1572868
  26.1 43.0 %collective-permute-start.4 = (bf16[8,256,128]{2,1,0:T(8,128)(2,1)S(1)}, bf16[8,256,128]{2,1,0:T(8,128)(2,1)}, u32[]{:S(2)}, u32[]{:S(2)}) collective-permute-start(bf16[8,256,128]{2,1,0:T(8,128)(2,1)S(1)} %collective-permute-done.2.refs_4_), channel_id=1, source_target_pairs={{0,112},{16,0},{32,16},{48,32},{64,48},{80,64},{96,80},{112,96},{1... | collective-permute-start | bytes 1572872 | tf_op jit(solution)/shard_map/ppermute | solution.py:142
  38.9 10.4 %copy-start.5 = (bf16[8,256,128]{2,1,0:T(8,128)(2,1)}, bf16[8,256,128]{2,1,0:T(8,128)(2,1)S(1)}, u32[]{:S(2)}) copy-start(bf16[8,256,128]{2,1,0:T(8,128)(2,1)S(1)} %collective-permute-done.3.refs_5_) | copy-start | bytes 1572868
  38.9 32.4 %collective-permute-start.5 = (bf16[8,256,128]{2,1,0:T(8,128)(2,1)S(1)}, bf16[8,256,128]{2,1,0:T(8,128)(2,1)}, u32[]{:S(2)}, u32[]{:S(2)}) collective-permute-start(bf16[8,256,128]{2,1,0:T(8,128)(2,1)S(1)} %collective-permute-done.3.refs_5_), channel_id=1, source_target_pairs={{0,16},{16,32},{32,48},{48,64},{64,80},{80,96},{96,112},{112,0},{1... | collective-permute-start | bytes 1572872 | tf_op jit(solution)/shard_map/ppermute | solution.py:140
  52.0 6.8 %copy-start.9 = (bf16[1,256,2048]{1,2,0:T(8,128)(2,1)S(1)}, bf16[1,256,2048]{1,2,0:T(8,128)(2,1)}, u32[]{:S(2)}) copy-start(bf16[1,256,2048]{1,2,0:T(8,128)(2,1)} %copy.27) | copy-start | bytes 3145732
  60.0 33.7 %collective-permute-start.10 = (bf16[8,256,128]{2,1,0:T(8,128)(2,1)S(1)}, bf16[8,256,128]{2,1,0:T(8,128)(2,1)S(1)}, u32[]{:S(2)}, u32[]{:S(2)}) collective-permute-start(bf16[8,256,128]{2,1,0:T(8,128)(2,1)S(1)} %collective-permute-done.2.refs_4_), channel_id=1, source_target_pairs={{0,128},{16,144},{32,160},{48,176},{64,192},{80,208},{96,224},{112... | collective-permute-start | bytes 1572872 | tf_op jit(solution)/shard_map/ppermute | solution.py:159
  61.3 51.0 %all-to-all-start.1 = ((bf16[16,8,4096]{2,1,0:T(8,128)(2,1)}), bf16[16,8,4096]{2,1,0:T(8,128)(2,1)}, u32[]{:S(2)}, u32[]{:S(2)}) async-start(bf16[16,8,4096]{2,1,0:T(8,128)(2,1)} %fusion.1), calls=%async_computation.1 | async-start | bytes 2097152 | tf_op jit(solution)/shard_map/all_to_all | solution.py:234
  67.9 29.4 %collective-permute-start.9 = (bf16[8,256,128]{2,1,0:T(8,128)(2,1)}, bf16[8,256,128]{2,1,0:T(8,128)(2,1)S(1)}, u32[]{:S(2)}, u32[]{:S(2)}) collective-permute-start(bf16[8,256,128]{2,1,0:T(8,128)(2,1)} %collective-permute-done.1.refs_3_), channel_id=1, source_target_pairs={{0,128},{16,144},{32,160},{48,176},{64,192},{80,208},{96,224},{112... | collective-permute-start | bytes 1572872 | tf_op jit(solution)/shard_map/ppermute | solution.py:159
  69.2 29.4 %collective-permute-start.6 = (bf16[8,256,128]{2,1,0:T(8,128)(2,1)}, bf16[8,256,128]{2,1,0:T(8,128)(2,1)}, u32[]{:S(2)}, u32[]{:S(2)}) collective-permute-start(bf16[8,256,128]{2,1,0:T(8,128)(2,1)} %collective-permute-done.4.refs_6_), channel_id=1, source_target_pairs={{0,112},{16,0},{32,16},{48,32},{64,48},{80,64},{96,80},{112,96},{1... | collective-permute-start | bytes 1572872 | tf_op jit(solution)/shard_map/ppermute | solution.py:142
  71.3 28.6 %collective-permute-start.7 = (bf16[8,256,128]{2,1,0:T(8,128)(2,1)}, bf16[8,256,128]{2,1,0:T(8,128)(2,1)}, u32[]{:S(2)}, u32[]{:S(2)}) collective-permute-start(bf16[8,256,128]{2,1,0:T(8,128)(2,1)} %collective-permute-done.5.refs_7_), channel_id=1, source_target_pairs={{0,16},{16,32},{32,48},{48,64},{64,80},{80,96},{96,112},{112,0},{1... | collective-permute-start | bytes 1572872 | tf_op jit(solution)/shard_map/ppermute | solution.py:140
  92.3 48.9 %collective-permute-start.11 = (bf16[8,256,128]{2,1,0:T(8,128)(2,1)}, bf16[8,256,128]{2,1,0:T(8,128)(2,1)S(1)}, u32[]{:S(2)}, u32[]{:S(2)}) collective-permute-start(bf16[8,256,128]{2,1,0:T(8,128)(2,1)} %copy-done.5), channel_id=1, source_target_pairs={{0,128},{16,144},{32,160},{48,176},{64,192},{80,208},{96,224},{112... | collective-permute-start | bytes 1572872 | tf_op jit(solution)/shard_map/ppermute | solution.py:159
  93.6 47.6 %collective-permute-start.12 = (bf16[8,256,128]{2,1,0:T(8,128)(2,1)}, bf16[8,256,128]{2,1,0:T(8,128)(2,1)S(1)}, u32[]{:S(2)}, u32[]{:S(2)}) collective-permute-start(bf16[8,256,128]{2,1,0:T(8,128)(2,1)} %collective-permute-done.4.refs_6_), channel_id=1, source_target_pairs={{0,128},{16,144},{32,160},{48,176},{64,192},{80,208},{96,224},{112... | collective-permute-start | bytes 1572872 | tf_op jit(solution)/shard_map/ppermute | solution.py:159
  97.2 62.7 %collective-permute-start.13 = (bf16[8,256,128]{2,1,0:T(8,128)(2,1)}, bf16[8,256,128]{2,1,0:T(8,128)(2,1)}, u32[]{:S(2)}, u32[]{:S(2)}) collective-permute-start(bf16[8,256,128]{2,1,0:T(8,128)(2,1)} %collective-permute-done.5.refs_7_), channel_id=1, source_target_pairs={{0,128},{16,144},{32,160},{48,176},{64,192},{80,208},{96,224},{112... | collective-permute-start | bytes 1572872 | tf_op jit(solution)/shard_map/ppermute | solution.py:159
  98.5 61.4 %collective-permute-start.14 = (bf16[8,256,128]{2,1,0:T(8,128)(2,1)}, bf16[8,256,128]{2,1,0:T(8,128)(2,1)}, u32[]{:S(2)}, u32[]{:S(2)}) collective-permute-start(bf16[8,256,128]{2,1,0:T(8,128)(2,1)} %collective-permute-done.6.refs_8_), channel_id=1, source_target_pairs={{0,128},{16,144},{32,160},{48,176},{64,192},{80,208},{96,224},{112... | collective-permute-start | bytes 1572872 | tf_op jit(solution)/shard_map/ppermute | solution.py:159
  99.8 60.1 %collective-permute-start.15 = (bf16[8,256,128]{2,1,0:T(8,128)(2,1)}, bf16[8,256,128]{2,1,0:T(8,128)(2,1)}, u32[]{:S(2)}, u32[]{:S(2)}) collective-permute-start(bf16[8,256,128]{2,1,0:T(8,128)(2,1)} %collective-permute-done.7.refs_9_), channel_id=1, source_target_pairs={{0,128},{16,144},{32,160},{48,176},{64,192},{80,208},{96,224},{112... | collective-permute-start | bytes 1572872 | tf_op jit(solution)/shard_map/ppermute | solution.py:159
  112.2 1.9 %copy-start.1 = (bf16[1,256,2048]{2,1,0:T(8,128)(2,1)S(1)}, bf16[1,256,2048]{2,1,0:T(8,128)(2,1)}, u32[]{:S(2)}) copy-start(bf16[1,256,2048]{2,1,0:T(8,128)(2,1)} %param.10) | copy-start | bytes 3145732
  112.2 1.9 %copy-start.4 = (bf16[8,256,128]{2,1,0:T(8,128)(2,1)S(1)}, bf16[8,256,128]{2,1,0:T(8,128)(2,1)}, u32[]{:S(2)}) copy-start(bf16[8,256,128]{2,1,0:T(8,128)(2,1)} %copy-done.3) | copy-start | bytes 1572868
  112.2 1.9 %copy-start.6 = (bf16[8,256,128]{2,1,0:T(8,128)(2,1)S(1)}, bf16[8,256,128]{2,1,0:T(8,128)(2,1)}, u32[]{:S(2)}) copy-start(bf16[8,256,128]{2,1,0:T(8,128)(2,1)} %copy-done.5) | copy-start | bytes 1572868
  158.6 1.3 copy-start.2
  160.0 12.2 %copy-start.8 = (f32[256,2048]{1,0:T(8,128)S(1)}, f32[256,2048]{1,0:T(8,128)}, u32[]{:S(2)}) copy-start(f32[256,2048]{1,0:T(8,128)} %copy.34) | copy-start | bytes 6291460
  160.0 12.2 %copy-start.10 = (bf16[1,256,2048]{2,1,0:T(8,128)(2,1)S(1)}, bf16[1,256,2048]{2,1,0:T(8,128)(2,1)}, u32[]{:S(2)}) copy-start(bf16[1,256,2048]{2,1,0:T(8,128)(2,1)} %param.14) | copy-start | bytes 3145732

commit v2 on v1

--- a/solution.py
+++ b/solution.py
@@ -136,9 +136,11 @@
     plus = [(r * ROW + z, r * ROW + (z + 1) % ROW) for r in range(rows) for z in range(ROW)]
     minus = [(r * ROW + z, r * ROW + (z - 1) % ROW) for r in range(rows) for z in range(ROW)]
     lefts, rights = [kv], [kv]
-    for _ in range(ROW // 2):
+    lefts.append(lax.ppermute(kv, "ctx", plus))
+    rights.append(lax.ppermute(kv, "ctx", minus))
+    for _ in range(ROW // 2 - 1):
         lefts.append(lax.ppermute(lefts[-1], "ctx", plus))
-    for _ in range(ROW - 1 - ROW // 2):
+    for _ in range(ROW - 2 - ROW // 2):
         rights.append(lax.ppermute(rights[-1], "ctx", minus))
     row_blocks = [kv]
     for k in range(1, max(len(lefts), len(rights))):
@@ -163,23 +165,23 @@
         return flash(jnp.stack(flags), query, blocks, None, True)
     state = flash(jnp.stack(flags[:split]), query, blocks[:split], None, False)
     late = split + len(row_blocks) - 3
+    last = len(blocks) - 1
     state = flash(jnp.stack(flags[split:late]), query, blocks[split:late], state, False)
-    return flash(jnp.stack(flags[late:]), query, blocks[late:], state, True)
+    state = flash(jnp.stack(flags[late:last]), query, blocks[late:last], state, False)
+    return flash(jnp.stack(flags[last:]), query, blocks[last:], state, True)
 
 
 def hyena_conv(first_in, value_in, filters, tok):
     width = first_in.shape[1]
     taps = filters.shape[1]
     fgroups = filters.shape[0]
+    lower, upper = circulant_parts(filters, taps)
     u_rows = (first_in.astype(jnp.float32) * value_in.astype(jnp.float32)).astype(jnp.bfloat16)
     before = passed_along(u_rows[tok - taps :], "ctx", 1)
-    return conv_body(before, u_rows, filters, tok, width, taps, fgroups)
-
-
-def conv_body(before, u_rows, filters, tok, width, taps, fgroups):
-    extended = jnp.concatenate([before, u_rows], 0)
-    nblk = tok // taps
-    blocks = extended.reshape(nblk + 1, taps, fgroups, width // fgroups)
+    return conv_body(before, u_rows, lower, upper, tok, width, taps, fgroups)
+
+
+def circulant_parts(filters, taps):
     rows_at = jnp.arange(taps, dtype=jnp.int32)
     lag = rows_at[:, None] - rows_at[None, :]
     wrapped = (lag + taps) % taps
@@ -190,6 +192,13 @@
     nothing = jnp.zeros((), jnp.bfloat16)
     lower = jnp.where((lag >= 0)[None], circulant, nothing)
     upper = jnp.where((lag < 0)[None], circulant, nothing)
+    return lower, upper
+
+
+def conv_body(before, u_rows, lower, upper, tok, width, taps, fgroups):
+    extended = jnp.concatenate([before, u_rows], 0)
+    nblk = tok // taps
+    blocks = extended.reshape(nblk + 1, taps, fgroups, width // fgroups)
     conv = jnp.einsum("gij,bjgc->bigc", lower, blocks[1:], preferred_element_type=jnp.float32)
     conv = conv + jnp.einsum(
         "gij,bjgc->bigc", upper, blocks[:-1], preferred_element_type=jnp.float32

time: 175 us -> 177 us (1.011)
  the two profiles are of different devices: /device:TPU:234 before, /device:TPU:254 now
where the time goes in v2:
time: 177 us; the launch traced here: 176 us
  Pallas kernels  56.9 us (32%)
  local copies, waits for them, and re-layouts  34.3 us (19%)
  starting transfers between devices  33.7 us (19%)
  matrix products  25.4 us (14%)
  waiting for transfers between devices  19.1 us (11%)
  other arithmetic  6.15 us (3%)
    pallas_call x4, Pallas kernels, flash(): pl.pallas_call(kernel, out_shape=out_shape, in_specs=[pl.BlockSpec(memory...  56.9 us
    ppermute x3, waiting for transfers between devices, attention(): lefts.append(lax.ppermute(lefts[-1], 'ctx', plus))  10.6 us
    ppermute x8, starting transfers between devices, attention(): blocks.append(lax.ppermute(piece, 'ctx', up))  10.5 us
    dot_general x1, matrix products, circulant_parts(): jnp.einsum('gk,kij->gij', filters, selector, preferred_element_type=jnp.f...  10.4 us
    all_to_all x1, starting transfers between devices, route_hints(): lax.all_to_all(buffer.reshape(dp_count, cap, entries), 'dp', split_axis=0...  7.21 us
    all_to_all x1, starting transfers between devices, route_hints(): lax.all_to_all(row_buffer.reshape(dp_count, cap), 'dp', split_axis=0, con...  7.2 us
    ppermute x1, waiting for transfers between devices, attention(): lefts.append(lax.ppermute(kv, 'ctx', plus))  7.02 us
    select_n x1, local copies, waits for them, and re-layouts, circulant_parts(): upper = jnp.where((lag < 0)[None], circulant, nothing)  6.7 us
  transfers between devices with their start and end apart: 18, of which 3 were waited for; matrix products, arithmetic and copies ran while one was open for 33% of the time, Pallas kernels for 30%

profile of v2, /device:TPU:254, one launch (start us, length us, event | category | flops | bytes accessed | tf_op | source)
XLA Modules:
  0.0 176.1 jit_solution(16697204919983013263)
XLA Ops:
  0.0 1.1 copy.35
  1.1 0.2 copy.37
  1.3 1.1 copy.36
  2.4 0.2 copy.38
  2.7 2.0 %collective-permute-start.2 = (bf16[8,256,128]{2,1,0:T(8,128)(2,1)S(1)}, bf16[8,256,128]{2,1,0:T(8,128)(2,1)S(1)}, u32[]{:S(2)}, u32[]{:S(2)}) collective-permute-start(bf16[8,256,128]{2,1,0:T(8,128)(2,1)S(1)} %maximum_bitcast_fusion.refs_2_), channel_id=1, source_target_pairs={{0,112},{16,0},{32,16},{48,32},{64,48},{80,64},{96,80},{112,96},{1... | collective-permute-start | bytes 1572872 | tf_op jit(solution)/shard_map/ppermute | solution.py:140
  4.8 1.3 collective-permute-start.8
  6.1 1.9 %multiply_convert_fusion = bf16[1,256,2048]{2,1,0:T(8,128)(2,1)S(1)} fusion(bf16[1,256,2048]{2,1,0:T(8,128)(2,1)} %param.15, bf16[1,256,2048]{2,1,0:T(8,128)(2,1)} %param.13), kind=kLoop, calls=%fused_computation.15 | loop fusion | flops 2097152 | bytes 3145728 | tf_op jit(solution)/shard_map/convert_element_type | solution.py:179
  8.0 1.0 copy-done.7
  9.1 1.3 collective-permute-start
  10.5 7.0 %collective-permute-done.1.refs_3_ = bf16[8,256,128]{2,1,0:T(8,128)(2,1)S(1)} collective-permute-done((bf16[8,256,128]{2,1,0:T(8,128)(2,1)S(1)}, bf16[8,256,128]{2,1,0:T(8,128)(2,1)S(1)}, u32[]{:S(2)}, u32[]{:S(2)}) %collective-permute-start.1) | collective-permute-done | bytes 524320 | tf_op jit(solution)/shard_map/ppermute | solution.py:139
  17.5 0.4 collective-permute-start.3
  17.9 0.8 scatter_custom_fusion
  18.7 0.7 all_to_all.9
  19.4 7.2 %all-to-all-start = ((s32[16,1,8]{2,1,0:T(1,128)}), s32[16,1,8]{2,1,0:T(1,128)S(1)}, u32[]{:S(2)}, u32[]{:S(2)}) async-start(s32[16,1,8]{2,1,0:T(1,128)} %bitcast.26), calls=%async_computation | async-start | bytes 16384 | tf_op jit(solution)/shard_map/all_to_all | solution.py:237
  26.7 1.7 collective-permute-start.4
  28.4 10.6 %collective-permute-done.3.refs_5_ = bf16[8,256,128]{2,1,0:T(8,128)(2,1)} collective-permute-done((bf16[8,256,128]{2,1,0:T(8,128)(2,1)S(1)}, bf16[8,256,128]{2,1,0:T(8,128)(2,1)}, u32[]{:S(2)}, u32[]{:S(2)}) %collective-permute-start.3) | collective-permute-done | bytes 524320 | tf_op jit(solution)/shard_map/ppermute | solution.py:142
  39.0 10.4 %select_bitcast_fusion = (bf16[128,128,128,1]{0,2,1,3:T(8,128)(2,1)}, bf16[128,128,128,1]{0,2,1,3:T(8,128)(2,1)}) fusion(pred[128,128]{1,0:T(8,128)(4,1)S(1)} %get-tuple-element.25, pred[128,128]{1,0:T(8,128)(4,1)S(1)} %get-tuple-element.26, bf16[128,128]{1,0:T(8,128)(2,1)S(1)} %copy-done.10, s32[128,128]{1,0:T(8,128)S(1)} %add_select_fusion), kind=kOutput, calls=%fused_computation.5 | convolution fusion | flops 545259520 | bytes 8519680 | tf_op jit(solution)/shard_map/gk,kij->gij/dot_general | solution.py:189
  49.4 1.4 fusion.1
  50.8 2.3 %copy.27 = bf16[1,256,2048]{1,2,0:T(8,128)(2,1)} copy(bf16[1,256,2048]{2,1,0:T(8,128)(2,1)} %copy-done.7) | data formatting | bytes 2097152 | tf_op jit(solution)/shard_map/convert_element_type | solution.py:179
  53.1 6.7 %copy.40 = bf16[128,128,128,1]{2,1,3,0:T(8,128)(2,1)} copy(bf16[128,128,128,1]{0,2,1,3:T(8,128)(2,1)} %get-tuple-element.24) | data formatting | bytes 8388608 | tf_op jit(solution)/shard_map/jit(_where)/select_n | solution.py:193
  59.8 2.2 %convert_element_type.74 = bf16[2,128,128,16]{1,0,3,2:T(2,128)(2,1)} reshape(bf16[1,256,2048]{1,2,0:T(8,128)(2,1)} %copy.27) | data formatting | bytes 2097152 | tf_op jit(solution)/shard_map/convert_element_type | solution.py:179
  62.0 1.3 collective-permute-start.10
  63.3 7.2 %all-to-all-start.1 = ((bf16[16,8,4096]{2,1,0:T(8,128)(2,1)}), bf16[16,8,4096]{2,1,0:T(8,128)(2,1)}, u32[]{:S(2)}, u32[]{:S(2)}) async-start(bf16[16,8,4096]{2,1,0:T(8,128)(2,1)} %fusion.1), calls=%async_computation.1 | async-start | bytes 2097152 | tf_op jit(solution)/shard_map/all_to_all | solution.py:243
  70.5 1.3 collective-permute-start.9
  71.8 2.1 %collective-permute-start.6 = (bf16[8,256,128]{2,1,0:T(8,128)(2,1)}, bf16[8,256,128]{2,1,0:T(8,128)(2,1)}, u32[]{:S(2)}, u32[]{:S(2)}) collective-permute-start(bf16[8,256,128]{2,1,0:T(8,128)(2,1)} %collective-permute-done.4.refs_6_), channel_id=1, source_target_pairs={{0,112},{16,0},{32,16},{48,32},{64,48},{80,64},{96,80},{112,96},{1... | collective-permute-start | bytes 1572872 | tf_op jit(solution)/shard_map/ppermute | solution.py:144
  73.9 1.2 collective-permute-start.7
  75.1 6.2 %fusion.10 = f32[128,2,16,128]{3,2,1,0:T(8,128)} fusion(bf16[128,128,128,1]{2,1,3,0:T(8,128)(2,1)} %copy.40, bf16[2,128,128,16]{1,0,3,2:T(2,128)(2,1)} %convert_element_type.74), kind=kOutput, calls=%fused_computation.21 | convolution fusion | flops 134217728 | bytes 7340032 | tf_op jit(solution)/shard_map/gij,bjgc->bigc/dot_general | solution.py:202
  81.4 6.7 %copy.41 = bf16[128,128,128,1]{2,1,3,0:T(8,128)(2,1)} copy(bf16[128,128,128,1]{0,2,1,3:T(8,128)(2,1)} %get-tuple-element.23) | data formatting | bytes 8388608 | tf_op jit(solution)/shard_map/jit(_where)/select_n | solution.py:194
  88.3 2.3 %pad_maximum_fusion = bf16[256,2048]{1,0:T(8,128)(2,1)} fusion(bf16[256,2048]{1,0:T(8,128)(2,1)} %bitcast.73, bf16[128,2048]{1,0:T(8,128)(2,1)} %collective-permute-done), kind=kLoop, calls=%fused_computation.19 | loop fusion | flops 2097152 | bytes 2621440 | tf_op jit(solution)/shard_map/concatenate | solution.py:199
  90.6 2.3 %copy.30 = bf16[256,2048]{0,1:T(8,128)(2,1)} copy(bf16[256,2048]{1,0:T(8,128)(2,1)} %pad_maximum_fusion) | data formatting | bytes 2097152 | tf_op jit(solution)/shard_map/slice | solution.py:204
  92.9 2.2 %slice.23 = bf16[2,128,128,16]{1,0,3,2:T(2,128)(2,1)} reshape(bf16[256,2048]{0,1:T(8,128)(2,1)} %copy.30) | data formatting | bytes 2097152 | tf_op jit(solution)/shard_map/slice | solution.py:204
  95.0 1.3 collective-permute-start.11
  96.3 1.3 collective-permute-start.12
  97.6 1.5 collective-permute-done.9.refs_6_
  99.1 1.3 collective-permute-start.13
  100.4 1.3 collective-permute-start.14
  101.7 1.5 collective-permute-start.15
  103.2 5.5 %add_bitcast_fusion = f32[2,128,128,16]{1,3,0,2:T(8,128)S(1)} fusion(f32[128,2,16,128]{3,2,1,0:T(8,128)} %fusion.10, bf16[128,128,128,1]{2,1,3,0:T(8,128)(2,1)} %copy.41, bf16[2,128,128,16]{1,0,3,2:T(2,128)(2,1)} %slice.23), kind=kOutput, calls=%fused_computation.14 | convolution fusion | flops 134742016 | bytes 9437184 | tf_op jit(solution)/shard_map/gij,bjgc->bigc/dot_general | solution.py:203
  108.7 1.1 copy.33
  109.8 1.4 copy.52
  111.2 2.9 %copy.34 = f32[256,2048]{1,0:T(8,128)} copy(f32[256,2048]{0,1:T(8,128)} %bitcast.75) | data formatting | bytes 4194304 | tf_op jit(solution)/shard_map/reshape | solution.py:206
  114.1 1.9 %fusion.12 = f32[256,2048]{1,0:T(8,128)S(1)} fusion(bf16[128,4096]{1,0:T(8,128)(2,1)} %bitcast.29, s32[128]{0:T(128)S(1)} %sub.71), kind=kOutput, calls=%fused_computation.24 | convolution fusion | flops 136085504 | bytes 3146240 | tf_op jit(solution)/shard_map/dot_general | solution.py:250
  116.0 27.1 %shard_map.100 = (f32[4,1,1024]{2,1,0:T(1,128)S(1)}, f32[4,1,1024]{2,1,0:T(1,128)S(1)}, f32[4,128,1024]{2,1,0:T(8,128)}) custom-call(s32[8]{0:T(128)S(1)} %stack.60.refs_0_, bf16[256,2048]{1,0:T(8,128)(2,1)S(1)} %bitcast.69, bf16[8,256,128]{2,1,0:T(8,128)(2,1)S(1)} %maximum_bitcast_fusion.refs_2_, bf16[8,256,128]{2,1,0:T(8,128)(2,1)S(1)} %copy-done.4, ...), custom_call_target="tpu_custom_call" | custom-call | tf_op jit(solution)/shard_map/pallas_call | solution.py:115
  143.1 17.6 %shard_map.101 = (f32[4,1,1024]{2,1,0:T(1,128)S(1)}, f32[4,1,1024]{2,1,0:T(1,128)S(1)}, f32[4,128,1024]{2,1,0:T(8,128)S(1)}) custom-call(s32[5]{0:T(128)S(1)} %stack.51.refs_0_, bf16[256,2048]{1,0:T(8,128)(2,1)S(1)} %bitcast.70, f32[4,1,1024]{2,1,0:T(1,128)S(1)} %get-tuple-element.14.refs_2_, f32[4,1,1024]{2,1,0:T(1,128)S(1)} %get-tuple-element.15.refs_3_, ...), custom_call_target="tpu_custom_call" | custom-call | tf_op jit(solution)/shard_map/pallas_call | solution.py:115
  160.8 1.3 copy-done.2
  162.1 8.2 %shard_map.102 = (f32[4,1,1024]{2,1,0:T(1,128)S(1)}, f32[4,1,1024]{2,1,0:T(1,128)S(1)}, f32[4,128,1024]{2,1,0:T(8,128)S(1)}) custom-call(s32[2]{0:T(128)S(1)} %pad_add_fusion.refs_0_, bf16[256,2048]{1,0:T(8,128)(2,1)S(1)} %bitcast.71, f32[4,1,1024]{2,1,0:T(1,128)S(1)} %get-tuple-element.17.refs_2_, f32[4,1,1024]{2,1,0:T(1,128)S(1)} %get-tuple-element.18.refs_3_, ...), custom_call_target="tpu_custom_call" | custom-call | tf_op jit(solution)/shard_map/pallas_call | solution.py:115
  170.3 4.0 %shard_map.103 = f32[256,2048]{1,0:T(8,128)S(1)} custom-call(s32[1]{0:T(128)} %bitcast.9.refs_0_, bf16[256,2048]{1,0:T(8,128)(2,1)S(1)} %bitcast.72, f32[4,1,1024]{2,1,0:T(1,128)S(1)} %get-tuple-element.20.refs_2_, f32[4,1,1024]{2,1,0:T(1,128)S(1)} %get-tuple-element.21.refs_3_, f32[4,128,1024]{2,1,0:T(8,128)S(1)} %get-tuple-element.22.refs_4_, ...), custom_call_target="tpu_custom_call" | custom-call | tf_op jit(solution)/shard_map/pallas_call | solution.py:115
  174.4 1.7 fusion.8
  (52 shorter events, 0.8 us)
Async XLA Ops:
  0.0 49.4 %copy-start = (bf16[1,32,4096]{2,1,0:T(8,128)(2,1)S(1)}, bf16[1,32,4096]{2,1,0:T(8,128)(2,1)}, u32[]{:S(2)}) copy-start(bf16[1,32,4096]{2,1,0:T(8,128)(2,1)} %param.17) | copy-start | bytes 786436
  2.6 7.7 %copy-start.11 = (s32[1,32,1]{1,2,0:T(1,128)S(1)}, s32[1,32,1]{1,2,0:T(1,128)}, u32[]{:S(2)}) copy-start(s32[1,32,1]{1,2,0:T(1,128)} %param.18) | copy-start | bytes 388
  2.6 36.4 %copy-start.10 = (bf16[128,128]{1,0:T(8,128)(2,1)S(1)}, bf16[128,128]{1,0:T(8,128)(2,1)}, u32[]{:S(2)}) copy-start(bf16[128,128]{1,0:T(8,128)(2,1)} %param.16) | copy-start | bytes 98308
  2.7 14.9 %collective-permute-start.1 = (bf16[8,256,128]{2,1,0:T(8,128)(2,1)S(1)}, bf16[8,256,128]{2,1,0:T(8,128)(2,1)S(1)}, u32[]{:S(2)}, u32[]{:S(2)}) collective-permute-start(bf16[8,256,128]{2,1,0:T(8,128)(2,1)S(1)} %maximum_bitcast_fusion.refs_2_), channel_id=1, source_target_pairs={{0,16},{16,32},{32,48},{48,64},{64,80},{80,96},{96,112},{112,0},{1... | collective-permute-start | bytes 1572872 | tf_op jit(solution)/shard_map/ppermute | solution.py:139
  2.7 23.9 %collective-permute-start.2 = (bf16[8,256,128]{2,1,0:T(8,128)(2,1)S(1)}, bf16[8,256,128]{2,1,0:T(8,128)(2,1)S(1)}, u32[]{:S(2)}, u32[]{:S(2)}) collective-permute-start(bf16[8,256,128]{2,1,0:T(8,128)(2,1)S(1)} %maximum_bitcast_fusion.refs_2_), channel_id=1, source_target_pairs={{0,112},{16,0},{32,16},{48,32},{64,48},{80,64},{96,80},{112,96},{1... | collective-permute-start | bytes 1572872 | tf_op jit(solution)/shard_map/ppermute | solution.py:140
  4.8 90.3 %collective-permute-start.8 = (bf16[8,256,128]{2,1,0:T(8,128)(2,1)S(1)}, bf16[8,256,128]{2,1,0:T(8,128)(2,1)S(1)}, u32[]{:S(2)}, u32[]{:S(2)}) collective-permute-start(bf16[8,256,128]{2,1,0:T(8,128)(2,1)S(1)} %maximum_bitcast_fusion.refs_2_), channel_id=1, source_target_pairs={{0,128},{16,144},{32,160},{48,176},{64,192},{80,208},{96,224},{112... | collective-permute-start | bytes 1572872 | tf_op jit(solution)/shard_map/ppermute | solution.py:161
  8.0 1.0 copy-start.7
  9.1 61.4 %collective-permute-start = (bf16[128,2048]{1,0:T(8,128)(2,1)S(1)}, bf16[128,2048]{1,0:T(8,128)(2,1)}, u32[]{:S(2)}, u32[]{:S(2)}) collective-permute-start(bf16[128,2048]{1,0:T(8,128)(2,1)S(1)} %slice_bitcast_fusion), channel_id=1, source_target_pairs={{0,16},{16,32},{32,48},{48,64},{64,80},{80,96},{96,112},{112,128},... | collective-permute-start | bytes 1572872 | tf_op jit(solution)/shard_map/ppermute | solution.py:21
  17.5 52.9 %copy-start.3 = (bf16[8,256,128]{2,1,0:T(8,128)(2,1)}, bf16[8,256,128]{2,1,0:T(8,128)(2,1)S(1)}, u32[]{:S(2)}) copy-start(bf16[8,256,128]{2,1,0:T(8,128)(2,1)S(1)} %collective-permute-done.1.refs_3_) | copy-start | bytes 1572868
  17.5 21.4 %collective-permute-start.3 = (bf16[8,256,128]{2,1,0:T(8,128)(2,1)S(1)}, bf16[8,256,128]{2,1,0:T(8,128)(2,1)}, u32[]{:S(2)}, u32[]{:S(2)}) collective-permute-start(bf16[8,256,128]{2,1,0:T(8,128)(2,1)S(1)} %collective-permute-done.1.refs_3_), channel_id=1, source_target_pairs={{0,16},{16,32},{32,48},{48,64},{64,80},{80,96},{96,112},{112,0},{1... | collective-permute-start | bytes 1572872 | tf_op jit(solution)/shard_map/ppermute | solution.py:142
  19.4 43.8 %all-to-all-start = ((s32[16,1,8]{2,1,0:T(1,128)}), s32[16,1,8]{2,1,0:T(1,128)S(1)}, u32[]{:S(2)}, u32[]{:S(2)}) async-start(s32[16,1,8]{2,1,0:T(1,128)} %bitcast.26), calls=%async_computation | async-start | bytes 16384 | tf_op jit(solution)/shard_map/all_to_all | solution.py:237
  26.7 35.3 %copy-start.5 = (bf16[8,256,128]{2,1,0:T(8,128)(2,1)}, bf16[8,256,128]{2,1,0:T(8,128)(2,1)S(1)}, u32[]{:S(2)}) copy-start(bf16[8,256,128]{2,1,0:T(8,128)(2,1)S(1)} %collective-permute-done.2.refs_4_) | copy-start | bytes 1572868
  26.7 45.1 %collective-permute-start.4 = (bf16[8,256,128]{2,1,0:T(8,128)(2,1)S(1)}, bf16[8,256,128]{2,1,0:T(8,128)(2,1)}, u32[]{:S(2)}, u32[]{:S(2)}) collective-permute-start(bf16[8,256,128]{2,1,0:T(8,128)(2,1)S(1)} %collective-permute-done.2.refs_4_), channel_id=1, source_target_pairs={{0,112},{16,0},{32,16},{48,32},{64,48},{80,64},{96,80},{112,96},{1... | collective-permute-start | bytes 1572872 | tf_op jit(solution)/shard_map/ppermute | solution.py:144
  39.0 34.9 %collective-permute-start.5 = (bf16[8,256,128]{2,1,0:T(8,128)(2,1)}, bf16[8,256,128]{2,1,0:T(8,128)(2,1)}, u32[]{:S(2)}, u32[]{:S(2)}) collective-permute-start(bf16[8,256,128]{2,1,0:T(8,128)(2,1)} %collective-permute-done.3.refs_5_), channel_id=1, source_target_pairs={{0,16},{16,32},{32,48},{48,64},{64,80},{80,96},{96,112},{112,0},{1... | collective-permute-start | bytes 1572872 | tf_op jit(solution)/shard_map/ppermute | solution.py:142
  62.0 34.4 %collective-permute-start.10 = (bf16[8,256,128]{2,1,0:T(8,128)(2,1)S(1)}, bf16[8,256,128]{2,1,0:T(8,128)(2,1)S(1)}, u32[]{:S(2)}, u32[]{:S(2)}) collective-permute-start(bf16[8,256,128]{2,1,0:T(8,128)(2,1)S(1)} %collective-permute-done.2.refs_4_), channel_id=1, source_target_pairs={{0,128},{16,144},{32,160},{48,176},{64,192},{80,208},{96,224},{112... | collective-permute-start | bytes 1572872 | tf_op jit(solution)/shard_map/ppermute | solution.py:161
  63.3 50.9 %all-to-all-start.1 = ((bf16[16,8,4096]{2,1,0:T(8,128)(2,1)}), bf16[16,8,4096]{2,1,0:T(8,128)(2,1)}, u32[]{:S(2)}, u32[]{:S(2)}) async-start(bf16[16,8,4096]{2,1,0:T(8,128)(2,1)} %fusion.1), calls=%async_computation.1 | async-start | bytes 2097152 | tf_op jit(solution)/shard_map/all_to_all | solution.py:243
  70.5 28.6 %collective-permute-start.9 = (bf16[8,256,128]{2,1,0:T(8,128)(2,1)S(1)}, bf16[8,256,128]{2,1,0:T(8,128)(2,1)S(1)}, u32[]{:S(2)}, u32[]{:S(2)}) collective-permute-start(bf16[8,256,128]{2,1,0:T(8,128)(2,1)S(1)} %collective-permute-done.1.refs_3_), channel_id=1, source_target_pairs={{0,128},{16,144},{32,160},{48,176},{64,192},{80,208},{96,224},{112... | collective-permute-start | bytes 1572872 | tf_op jit(solution)/shard_map/ppermute | solution.py:161
  71.8 28.6 %collective-permute-start.6 = (bf16[8,256,128]{2,1,0:T(8,128)(2,1)}, bf16[8,256,128]{2,1,0:T(8,128)(2,1)}, u32[]{:S(2)}, u32[]{:S(2)}) collective-permute-start(bf16[8,256,128]{2,1,0:T(8,128)(2,1)} %collective-permute-done.4.refs_6_), channel_id=1, source_target_pairs={{0,112},{16,0},{32,16},{48,32},{64,48},{80,64},{96,80},{112,96},{1... | collective-permute-start | bytes 1572872 | tf_op jit(solution)/shard_map/ppermute | solution.py:144
  73.9 27.8 %collective-permute-start.7 = (bf16[8,256,128]{2,1,0:T(8,128)(2,1)}, bf16[8,256,128]{2,1,0:T(8,128)(2,1)}, u32[]{:S(2)}, u32[]{:S(2)}) collective-permute-start(bf16[8,256,128]{2,1,0:T(8,128)(2,1)} %collective-permute-done.5.refs_7_), channel_id=1, source_target_pairs={{0,16},{16,32},{32,48},{48,64},{64,80},{80,96},{96,112},{112,0},{1... | collective-permute-start | bytes 1572872 | tf_op jit(solution)/shard_map/ppermute | solution.py:142
  95.0 48.1 %collective-permute-start.11 = (bf16[8,256,128]{2,1,0:T(8,128)(2,1)}, bf16[8,256,128]{2,1,0:T(8,128)(2,1)}, u32[]{:S(2)}, u32[]{:S(2)}) collective-permute-start(bf16[8,256,128]{2,1,0:T(8,128)(2,1)} %collective-permute-done.3.refs_5_), channel_id=1, source_target_pairs={{0,128},{16,144},{32,160},{48,176},{64,192},{80,208},{96,224},{112... | collective-permute-start | bytes 1572872 | tf_op jit(solution)/shard_map/ppermute | solution.py:161
  96.3 46.8 %collective-permute-start.12 = (bf16[8,256,128]{2,1,0:T(8,128)(2,1)}, bf16[8,256,128]{2,1,0:T(8,128)(2,1)}, u32[]{:S(2)}, u32[]{:S(2)}) collective-permute-start(bf16[8,256,128]{2,1,0:T(8,128)(2,1)} %collective-permute-done.4.refs_6_), channel_id=1, source_target_pairs={{0,128},{16,144},{32,160},{48,176},{64,192},{80,208},{96,224},{112... | collective-permute-start | bytes 1572872 | tf_op jit(solution)/shard_map/ppermute | solution.py:161
  99.1 62.9 %collective-permute-start.13 = (bf16[8,256,128]{2,1,0:T(8,128)(2,1)}, bf16[8,256,128]{2,1,0:T(8,128)(2,1)S(1)}, u32[]{:S(2)}, u32[]{:S(2)}) collective-permute-start(bf16[8,256,128]{2,1,0:T(8,128)(2,1)} %collective-permute-done.5.refs_7_), channel_id=1, source_target_pairs={{0,128},{16,144},{32,160},{48,176},{64,192},{80,208},{96,224},{112... | collective-permute-start | bytes 1572872 | tf_op jit(solution)/shard_map/ppermute | solution.py:161
  100.4 61.6 %collective-permute-start.14 = (bf16[8,256,128]{2,1,0:T(8,128)(2,1)}, bf16[8,256,128]{2,1,0:T(8,128)(2,1)}, u32[]{:S(2)}, u32[]{:S(2)}) collective-permute-start(bf16[8,256,128]{2,1,0:T(8,128)(2,1)} %collective-permute-done.6.refs_8_), channel_id=1, source_target_pairs={{0,128},{16,144},{32,160},{48,176},{64,192},{80,208},{96,224},{112... | collective-permute-start | bytes 1572872 | tf_op jit(solution)/shard_map/ppermute | solution.py:161
  101.7 68.6 %collective-permute-start.15 = (bf16[8,256,128]{2,1,0:T(8,128)(2,1)}, bf16[8,256,128]{2,1,0:T(8,128)(2,1)S(1)}, u32[]{:S(2)}, u32[]{:S(2)}) collective-permute-start(bf16[8,256,128]{2,1,0:T(8,128)(2,1)} %collective-permute-done.7.refs_9_), channel_id=1, source_target_pairs={{0,128},{16,144},{32,160},{48,176},{64,192},{80,208},{96,224},{112... | collective-permute-start | bytes 1572872 | tf_op jit(solution)/shard_map/ppermute | solution.py:161
  114.1 1.9 %copy-start.1 = (bf16[1,256,2048]{2,1,0:T(8,128)(2,1)S(1)}, bf16[1,256,2048]{2,1,0:T(8,128)(2,1)}, u32[]{:S(2)}) copy-start(bf16[1,256,2048]{2,1,0:T(8,128)(2,1)} %param.10) | copy-start | bytes 3145732
  114.1 1.9 %copy-start.4 = (bf16[8,256,128]{2,1,0:T(8,128)(2,1)S(1)}, bf16[8,256,128]{2,1,0:T(8,128)(2,1)}, u32[]{:S(2)}) copy-start(bf16[8,256,128]{2,1,0:T(8,128)(2,1)} %copy-done.3) | copy-start | bytes 1572868
  114.1 1.9 %copy-start.6 = (bf16[8,256,128]{2,1,0:T(8,128)(2,1)S(1)}, bf16[8,256,128]{2,1,0:T(8,128)(2,1)}, u32[]{:S(2)}) copy-start(bf16[8,256,128]{2,1,0:T(8,128)(2,1)} %copy-done.5) | copy-start | bytes 1572868
  160.7 1.3 copy-start.2
  170.3 4.0 %copy-start.8 = (f32[256,2048]{1,0:T(8,128)S(1)}, f32[256,2048]{1,0:T(8,128)}, u32[]{:S(2)}) copy-start(f32[256,2048]{1,0:T(8,128)} %copy.34) | copy-start | bytes 6291460
  170.3 4.0 %copy-start.9 = (bf16[1,256,2048]{2,1,0:T(8,128)(2,1)S(1)}, bf16[1,256,2048]{2,1,0:T(8,128)(2,1)}, u32[]{:S(2)}) copy-start(bf16[1,256,2048]{2,1,0:T(8,128)(2,1)} %param.14) | copy-start | bytes 3145732

commit v3 on v2

--- a/solution.py
+++ b/solution.py
@@ -163,7 +163,8 @@
     split = len(row_blocks)
     if split == len(blocks):
         return flash(jnp.stack(flags), query, blocks, None, True)
-    state = flash(jnp.stack(flags[:split]), query, blocks[:split], None, False)
+    state = flash(jnp.stack(flags[:3]), query, blocks[:3], None, False)
+    state = flash(jnp.stack(flags[3:split]), query, blocks[3:split], state, False)
     late = split + len(row_blocks) - 3
     last = len(blocks) - 1
     state = flash(jnp.stack(flags[split:late]), query, blocks[split:late], state, False)
@@ -232,18 +233,16 @@
     earlier = jnp.sum(jnp.dot(before_mask, marks) * marks, axis=1)
     slots = owners * cap + earlier
     base_row = ctx_index * tok
-    row_buffer = jnp.full((dp_count * cap,), base_row, jnp.int32).at[slots].set(step_rows[0])
-    arrived_rows = (
-        lax.all_to_all(
-            row_buffer.reshape(dp_count, cap), "dp", split_axis=0, concat_axis=0, tiled=True
-        ).reshape(dp_count * cap)
-        - base_row
-    )
-    buffer = place_rows(slots, panels[0], dp_count * cap)
+    offsets = (step_rows[0] - base_row).astype(jnp.bfloat16)
+    lanes = jnp.arange(128, dtype=jnp.int32)[None, :] == 0
+    offset_cols = jnp.where(lanes, offsets[:, None], jnp.zeros((), jnp.bfloat16))
+    rows_ext = jnp.concatenate([panels[0], offset_cols], axis=1)
+    buffer = place_rows(slots, rows_ext, dp_count * cap)
     received = lax.all_to_all(
-        buffer.reshape(dp_count, cap, entries), "dp", split_axis=0, concat_axis=0, tiled=True
-    )
-    arrived = blend(received.reshape(dp_count * cap, entries), width)
+        buffer.reshape(dp_count, cap, entries + 128), "dp", split_axis=0, concat_axis=0, tiled=True
+    ).reshape(dp_count * cap, entries + 128)
+    arrived_rows = received[:, entries].astype(jnp.int32)
+    arrived = blend(received[:, :entries], width)
     landing = (jnp.arange(tok, dtype=jnp.int32)[:, None] == arrived_rows[None, :]).astype(
         jnp.bfloat16
     )

time: 177 us -> 177 us (level)
  starting transfers between devices: 33.7 us -> 26.6 us
  waiting for transfers between devices: 19.1 us -> 23.1 us
  Pallas kernels: 56.9 us -> 59.1 us
    all_to_all x2 -> x1, starting transfers between devices: 14.4 us -> 7.2 us  [route_hints(): lax.all_to_all(buffer.reshape(dp_count, cap, entries + 128), 'dp', split_...]
    ppermute x8, waiting for transfers between devices: 1.49 us -> 6.92 us  [attention(): blocks.append(lax.ppermute(piece, 'ctx', up))]
    unnamed x27 -> x41, local copies, waits for them, and re-layouts: 6 us -> 8.76 us
    pallas_call x4 -> x5, Pallas kernels: 56.9 us -> 59.1 us  [flash(): pl.pallas_call(kernel, out_shape=out_shape, in_specs=[pl.BlockSpec(memory...]
    convert_element_type x2, local copies, waits for them, and re-layouts: 4.44 us -> 2.4 us  [hyena_conv(): (first_in.astype(jnp.float32) * value_in.astype(jnp.float32)).astype(jnp....]
  transfers between devices with their start and end apart: 18 -> 17, of which waited for: 3 -> 3; matrix products, arithmetic and copies ran while one was open for 33% -> 33% of each run, Pallas kernels for 30% -> 31%
where the time goes in v3:
time: 177 us; the launch traced here: 176 us
  Pallas kernels  59.1 us (33%)
  local copies, waits for them, and re-layouts  34.5 us (19%)
  starting transfers between devices  26.6 us (15%)
  matrix products  25.3 us (14%)
  waiting for transfers between devices  23.1 us (13%)
  other arithmetic  6.96 us (4%)
    pallas_call x5, Pallas kernels, flash(): pl.pallas_call(kernel, out_shape=out_shape, in_specs=[pl.BlockSpec(memory...  59.1 us
    ppermute x8, starting transfers between devices, attention(): blocks.append(lax.ppermute(piece, 'ctx', up))  10.6 us
    dot_general x1, matrix products, circulant_parts(): jnp.einsum('gk,kij->gij', filters, selector, preferred_element_type=jnp.f...  10.4 us
    ppermute x3, waiting for transfers between devices, attention(): lefts.append(lax.ppermute(lefts[-1], 'ctx', plus))  9.09 us
    unnamed x41, local copies, waits for them, and re-layouts  8.76 us
    all_to_all x1, starting transfers between devices, route_hints(): lax.all_to_all(buffer.reshape(dp_count, cap, entries + 128), 'dp', split_...  7.2 us
    ppermute x1, waiting for transfers between devices, attention(): lefts.append(lax.ppermute(kv, 'ctx', plus))  7.08 us
    ppermute x8, waiting for transfers between devices, attention(): blocks.append(lax.ppermute(piece, 'ctx', up))  6.92 us
  transfers between devices with their start and end apart: 17, of which 3 were waited for; matrix products, arithmetic and copies ran while one was open for 33% of the time, Pallas kernels for 31%

profile of v3, /device:TPU:254, one launch (start us, length us, event | category | flops | bytes accessed | tf_op | source)
XLA Modules:
  0.0 176.0 jit_solution(6130777913810640787)
XLA Ops:
  0.0 1.1 copy.36
  1.3 1.1 copy.37
  2.7 2.0 %collective-permute-start.2 = (bf16[8,256,128]{2,1,0:T(8,128)(2,1)S(1)}, bf16[8,256,128]{2,1,0:T(8,128)(2,1)}, u32[]{:S(2)}, u32[]{:S(2)}) collective-permute-start(bf16[8,256,128]{2,1,0:T(8,128)(2,1)S(1)} %maximum_bitcast_fusion.refs_2_), channel_id=1, source_target_pairs={{0,112},{16,0},{32,16},{48,32},{64,48},{80,64},{96,80},{112,96},{1... | collective-permute-start | bytes 1572872 | tf_op jit(solution)/shard_map/ppermute | solution.py:140
  4.7 1.3 collective-permute-start.8
  6.0 1.9 %multiply_convert_fusion = bf16[1,256,2048]{2,1,0:T(8,128)(2,1)S(1)} fusion(bf16[1,256,2048]{2,1,0:T(8,128)(2,1)} %param.15, bf16[1,256,2048]{2,1,0:T(8,128)(2,1)} %param.13), kind=kLoop, calls=%fused_computation.14 | loop fusion | flops 2097152 | bytes 3145728 | tf_op jit(solution)/shard_map/convert_element_type | solution.py:180
  8.0 0.9 slice_bitcast_fusion
  8.9 1.3 collective-permute-start
  10.4 7.1 %collective-permute-done.1.refs_3_ = bf16[8,256,128]{2,1,0:T(8,128)(2,1)S(1)} collective-permute-done((bf16[8,256,128]{2,1,0:T(8,128)(2,1)S(1)}, bf16[8,256,128]{2,1,0:T(8,128)(2,1)S(1)}, u32[]{:S(2)}, u32[]{:S(2)}) %collective-permute-start.1) | collective-permute-done | bytes 524320 | tf_op jit(solution)/shard_map/ppermute | solution.py:139
  17.5 0.4 collective-permute-start.3
  17.9 1.4 fusion.1
  19.3 7.2 %all-to-all-start = ((bf16[16,8,4224]{2,1,0:T(8,128)(2,1)}), bf16[16,8,4224]{2,1,0:T(8,128)(2,1)}, u32[]{:S(2)}, u32[]{:S(2)}) async-start(bf16[16,8,4224]{2,1,0:T(8,128)(2,1)} %fusion.1), calls=%async_computation | async-start | bytes 2162688 | tf_op jit(solution)/shard_map/all_to_all | solution.py:241
  26.5 1.3 copy.28
  28.0 1.7 collective-permute-start.4
  29.8 9.1 %collective-permute-done.3.refs_5_ = bf16[8,256,128]{2,1,0:T(8,128)(2,1)S(1)} collective-permute-done((bf16[8,256,128]{2,1,0:T(8,128)(2,1)S(1)}, bf16[8,256,128]{2,1,0:T(8,128)(2,1)S(1)}, u32[]{:S(2)}, u32[]{:S(2)}) %collective-permute-start.3) | collective-permute-done | bytes 524320 | tf_op jit(solution)/shard_map/ppermute | solution.py:142
  38.9 10.4 %select_bitcast_fusion = (bf16[128,128,128,1]{0,2,1,3:T(8,128)(2,1)}, bf16[128,128,128,1]{0,2,1,3:T(8,128)(2,1)}) fusion(pred[128,128]{1,0:T(8,128)(4,1)S(1)} %get-tuple-element.31, pred[128,128]{1,0:T(8,128)(4,1)S(1)} %get-tuple-element.32, bf16[128,128]{1,0:T(8,128)(2,1)S(1)} %copy-done, s32[128,128]{1,0:T(8,128)S(1)} %add_select_fusion), kind=kOutput, calls=%fused_computation.4 | convolution fusion | flops 545259520 | bytes 8519680 | tf_op jit(solution)/shard_map/gk,kij->gij/dot_general | solution.py:190
  49.2 6.8 %copy.40 = bf16[128,128,128,1]{2,1,3,0:T(8,128)(2,1)} copy(bf16[128,128,128,1]{0,2,1,3:T(8,128)(2,1)} %get-tuple-element.30) | data formatting | bytes 8388608 | tf_op jit(solution)/shard_map/jit(_where)/select_n | solution.py:194
  56.1 1.1 convert_element_type.94
  57.1 6.7 %copy.41 = bf16[128,128,128,1]{2,1,3,0:T(8,128)(2,1)} copy(bf16[128,128,128,1]{0,2,1,3:T(8,128)(2,1)} %get-tuple-element.29) | data formatting | bytes 8388608 | tf_op jit(solution)/shard_map/jit(_where)/select_n | solution.py:195
  64.0 1.4 collective-permute-start.10
  65.4 1.3 collective-permute-start.9
  66.7 2.1 %collective-permute-start.6 = (bf16[8,256,128]{2,1,0:T(8,128)(2,1)}, bf16[8,256,128]{2,1,0:T(8,128)(2,1)}, u32[]{:S(2)}, u32[]{:S(2)}) collective-permute-start(bf16[8,256,128]{2,1,0:T(8,128)(2,1)} %collective-permute-done.4.refs_6_), channel_id=1, source_target_pairs={{0,112},{16,0},{32,16},{48,32},{64,48},{80,64},{96,80},{112,96},{1... | collective-permute-start | bytes 1572872 | tf_op jit(solution)/shard_map/ppermute | solution.py:144
  68.8 1.2 collective-permute-start.7
  70.0 6.2 %fusion.10 = f32[128,2,16,128]{3,2,1,0:T(8,128)} fusion(bf16[128,128,128,1]{2,1,3,0:T(8,128)(2,1)} %copy.40, bf16[2,128,128,16]{1,0,3,2:T(2,128)(2,1)} %convert_element_type.94), kind=kOutput, calls=%fused_computation.20 | convolution fusion | flops 134217728 | bytes 7340032 | tf_op jit(solution)/shard_map/gij,bjgc->bigc/dot_general | solution.py:203
  76.2 2.1 %pad_maximum_fusion = bf16[256,2048]{1,0:T(8,128)(2,1)} fusion(bf16[256,2048]{1,0:T(8,128)(2,1)S(1)} %bitcast.64, bf16[128,2048]{1,0:T(8,128)(2,1)} %collective-permute-done), kind=kLoop, calls=%fused_computation.18 | loop fusion | flops 2097152 | bytes 2621440 | tf_op jit(solution)/shard_map/concatenate | solution.py:200
  78.4 2.2 %copy.31 = bf16[256,2048]{0,1:T(8,128)(2,1)} copy(bf16[256,2048]{1,0:T(8,128)(2,1)} %pad_maximum_fusion) | data formatting | bytes 2097152 | tf_op jit(solution)/shard_map/slice | solution.py:205
  80.6 2.1 %slice.29 = bf16[2,128,128,16]{1,0,3,2:T(2,128)(2,1)} reshape(bf16[256,2048]{0,1:T(8,128)(2,1)} %copy.31) | data formatting | bytes 2097152 | tf_op jit(solution)/shard_map/slice | solution.py:205
  82.7 1.3 collective-permute-start.11
  84.0 1.3 collective-permute-start.12
  85.3 6.9 %collective-permute-done.9.refs_6_ = bf16[8,256,128]{2,1,0:T(8,128)(2,1)S(1)} collective-permute-done((bf16[8,256,128]{2,1,0:T(8,128)(2,1)}, bf16[8,256,128]{2,1,0:T(8,128)(2,1)S(1)}, u32[]{:S(2)}, u32[]{:S(2)}) %collective-permute-start.9) | collective-permute-done | bytes 524320 | tf_op jit(solution)/shard_map/ppermute | solution.py:161
  92.2 1.3 collective-permute-start.13
  93.5 1.3 collective-permute-start.14
  94.9 1.5 collective-permute-start.15
  96.3 5.5 %add_bitcast_fusion = f32[2,128,128,16]{1,3,0,2:T(8,128)S(1)} fusion(f32[128,2,16,128]{3,2,1,0:T(8,128)} %fusion.10, bf16[128,128,128,1]{2,1,3,0:T(8,128)(2,1)} %copy.41, bf16[2,128,128,16]{1,0,3,2:T(2,128)(2,1)} %slice.29), kind=kOutput, calls=%fused_computation.13 | convolution fusion | flops 134742016 | bytes 9437184 | tf_op jit(solution)/shard_map/gij,bjgc->bigc/dot_general | solution.py:204
  101.8 1.1 copy.34
  102.9 1.5 copy.52
  104.4 3.0 %copy.35 = f32[256,2048]{1,0:T(8,128)} copy(f32[256,2048]{0,1:T(8,128)} %bitcast.66) | data formatting | bytes 4194304 | tf_op jit(solution)/shard_map/reshape | solution.py:207
  107.4 1.0 copy-done.10
  108.4 10.2 %shard_map.100 = (f32[4,1,1024]{2,1,0:T(1,128)S(1)}, f32[4,1,1024]{2,1,0:T(1,128)S(1)}, f32[4,128,1024]{2,1,0:T(8,128)S(1)}) custom-call(s32[3]{0:T(128)S(1)} %add_convert_fusion.refs_0_, bf16[256,2048]{1,0:T(8,128)(2,1)S(1)} %bitcast.59, bf16[8,256,128]{2,1,0:T(8,128)(2,1)S(1)} %maximum_bitcast_fusion.refs_2_, bf16[8,256,128]{2,1,0:T(8,128)(2,1)S(1)} %copy-done.10, ...), custom_call_target="tpu_custom_call" | custom-call | tf_op jit(solution)/shard_map/pallas_call | solution.py:115
  118.7 1.3 copy-done.3
  120.0 0.9 convert_reduce_fusion
  120.9 1.7 fusion.12
  122.6 17.6 %shard_map.101 = (f32[4,1,1024]{2,1,0:T(1,128)S(1)}, f32[4,1,1024]{2,1,0:T(1,128)S(1)}, f32[4,128,1024]{2,1,0:T(8,128)S(1)}) custom-call(s32[5]{0:T(128)S(1)} %stack.63.refs_0_, bf16[256,2048]{1,0:T(8,128)(2,1)S(1)} %bitcast.60, f32[4,1,1024]{2,1,0:T(1,128)S(1)} %get-tuple-element.17.refs_2_, f32[4,1,1024]{2,1,0:T(1,128)S(1)} %get-tuple-element.18.refs_3_, ...), custom_call_target="tpu_custom_call" | custom-call | tf_op jit(solution)/shard_map/pallas_call | solution.py:115
  140.3 1.3 copy-done.2
  141.6 17.6 %shard_map.102 = (f32[4,1,1024]{2,1,0:T(1,128)S(1)}, f32[4,1,1024]{2,1,0:T(1,128)S(1)}, f32[4,128,1024]{2,1,0:T(8,128)S(1)}) custom-call(s32[5]{0:T(128)S(1)} %stack.56.refs_0_, bf16[256,2048]{1,0:T(8,128)(2,1)S(1)} %bitcast.61, f32[4,1,1024]{2,1,0:T(1,128)S(1)} %get-tuple-element.20.refs_2_, f32[4,1,1024]{2,1,0:T(1,128)S(1)} %get-tuple-element.21.refs_3_, ...), custom_call_target="tpu_custom_call" | custom-call | tf_op jit(solution)/shard_map/pallas_call | solution.py:115
  159.2 1.3 copy-done.4
  160.6 8.4 %shard_map.103 = (f32[4,1,1024]{2,1,0:T(1,128)S(1)}, f32[4,1,1024]{2,1,0:T(1,128)S(1)}, f32[4,128,1024]{2,1,0:T(8,128)S(1)}) custom-call(s32[2]{0:T(128)S(1)} %pad_add_fusion.refs_0_, bf16[256,2048]{1,0:T(8,128)(2,1)S(1)} %bitcast.62, f32[4,1,1024]{2,1,0:T(1,128)S(1)} %get-tuple-element.23.refs_2_, f32[4,1,1024]{2,1,0:T(1,128)S(1)} %get-tuple-element.24.refs_3_, ...), custom_call_target="tpu_custom_call" | custom-call | tf_op jit(solution)/shard_map/pallas_call | solution.py:115
  169.0 5.3 %shard_map.104 = f32[256,2048]{1,0:T(8,128)S(1)} custom-call(s32[1]{0:T(128)} %bitcast.9.refs_0_, bf16[256,2048]{1,0:T(8,128)(2,1)S(1)} %bitcast.63, f32[4,1,1024]{2,1,0:T(1,128)S(1)} %get-tuple-element.26.refs_2_, f32[4,1,1024]{2,1,0:T(1,128)S(1)} %get-tuple-element.27.refs_3_, f32[4,128,1024]{2,1,0:T(8,128)S(1)} %get-tuple-element.28.refs_4_, ...), custom_call_target="tpu_custom_call" | custom-call | tf_op jit(solution)/shard_map/pallas_call | solution.py:115
  174.3 1.7 fusion.8
  (65 shorter events, 1.1 us)
Async XLA Ops:
  0.0 38.9 %copy-start = (bf16[128,128]{1,0:T(8,128)(2,1)S(1)}, bf16[128,128]{1,0:T(8,128)(2,1)}, u32[]{:S(2)}) copy-start(bf16[128,128]{1,0:T(8,128)(2,1)} %param.16) | copy-start | bytes 98308
  2.6 7.6 %copy-start.18 = (s32[1,32,1]{1,2,0:T(1,128)S(1)}, s32[1,32,1]{1,2,0:T(1,128)}, u32[]{:S(2)}) copy-start(s32[1,32,1]{1,2,0:T(1,128)} %param.18) | copy-start | bytes 388
  2.6 7.7 %copy-start.17 = (s32[1,32]{1,0:T(1,128)S(1)}, s32[1,32]{1,0:T(1,128)}, u32[]{:S(2)}) copy-start(s32[1,32]{1,0:T(1,128)} %param.19) | copy-start | bytes 388
  2.6 15.3 %copy-start.16 = (bf16[1,32,4096]{2,1,0:T(8,128)(2,1)S(1)}, bf16[1,32,4096]{2,1,0:T(8,128)(2,1)}, u32[]{:S(2)}) copy-start(bf16[1,32,4096]{2,1,0:T(8,128)(2,1)} %param.17) | copy-start | bytes 786436
  2.6 14.9 %collective-permute-start.1 = (bf16[8,256,128]{2,1,0:T(8,128)(2,1)S(1)}, bf16[8,256,128]{2,1,0:T(8,128)(2,1)S(1)}, u32[]{:S(2)}, u32[]{:S(2)}) collective-permute-start(bf16[8,256,128]{2,1,0:T(8,128)(2,1)S(1)} %maximum_bitcast_fusion.refs_2_), channel_id=1, source_target_pairs={{0,16},{16,32},{32,48},{48,64},{64,80},{80,96},{96,112},{112,0},{1... | collective-permute-start | bytes 1572872 | tf_op jit(solution)/shard_map/ppermute | solution.py:139
  2.7 25.3 %collective-permute-start.2 = (bf16[8,256,128]{2,1,0:T(8,128)(2,1)S(1)}, bf16[8,256,128]{2,1,0:T(8,128)(2,1)}, u32[]{:S(2)}, u32[]{:S(2)}) collective-permute-start(bf16[8,256,128]{2,1,0:T(8,128)(2,1)S(1)} %maximum_bitcast_fusion.refs_2_), channel_id=1, source_target_pairs={{0,112},{16,0},{32,16},{48,32},{64,48},{80,64},{96,80},{112,96},{1... | collective-permute-start | bytes 1572872 | tf_op jit(solution)/shard_map/ppermute | solution.py:140
  4.7 78.0 %collective-permute-start.8 = (bf16[8,256,128]{2,1,0:T(8,128)(2,1)S(1)}, bf16[8,256,128]{2,1,0:T(8,128)(2,1)S(1)}, u32[]{:S(2)}, u32[]{:S(2)}) collective-permute-start(bf16[8,256,128]{2,1,0:T(8,128)(2,1)S(1)} %maximum_bitcast_fusion.refs_2_), channel_id=1, source_target_pairs={{0,128},{16,144},{32,160},{48,176},{64,192},{80,208},{96,224},{112... | collective-permute-start | bytes 1572872 | tf_op jit(solution)/shard_map/ppermute | solution.py:161
  8.0 18.5 %copy-start.11 = (bf16[1,256,2048]{2,1,0:T(8,128)(2,1)}, bf16[1,256,2048]{2,1,0:T(8,128)(2,1)S(1)}, u32[]{:S(2)}) copy-start(bf16[1,256,2048]{2,1,0:T(8,128)(2,1)S(1)} %multiply_convert_fusion) | copy-start | bytes 3145732
  8.9 56.5 %collective-permute-start = (bf16[128,2048]{1,0:T(8,128)(2,1)}, bf16[128,2048]{1,0:T(8,128)(2,1)}, u32[]{:S(2)}, u32[]{:S(2)}) collective-permute-start(bf16[128,2048]{1,0:T(8,128)(2,1)} %slice_bitcast_fusion), channel_id=1, source_target_pairs={{0,16},{16,32},{32,48},{48,64},{64,80},{80,96},{96,112},{112,128},... | collective-permute-start | bytes 1572872 | tf_op jit(solution)/shard_map/ppermute | solution.py:21
  17.5 10.3 %copy-start.9 = (bf16[8,256,128]{2,1,0:T(8,128)(2,1)}, bf16[8,256,128]{2,1,0:T(8,128)(2,1)S(1)}, u32[]{:S(2)}) copy-start(bf16[8,256,128]{2,1,0:T(8,128)(2,1)S(1)} %collective-permute-done.1.refs_3_) | copy-start | bytes 1572868
  17.5 21.3 %collective-permute-start.3 = (bf16[8,256,128]{2,1,0:T(8,128)(2,1)S(1)}, bf16[8,256,128]{2,1,0:T(8,128)(2,1)S(1)}, u32[]{:S(2)}, u32[]{:S(2)}) collective-permute-start(bf16[8,256,128]{2,1,0:T(8,128)(2,1)S(1)} %collective-permute-done.1.refs_3_), channel_id=1, source_target_pairs={{0,16},{16,32},{32,48},{48,64},{64,80},{80,96},{96,112},{112,0},{1... | collective-permute-start | bytes 1572872 | tf_op jit(solution)/shard_map/ppermute | solution.py:142
  19.3 100.7 %all-to-all-start = ((bf16[16,8,4224]{2,1,0:T(8,128)(2,1)}), bf16[16,8,4224]{2,1,0:T(8,128)(2,1)}, u32[]{:S(2)}, u32[]{:S(2)}) async-start(bf16[16,8,4224]{2,1,0:T(8,128)(2,1)} %fusion.1), calls=%async_computation | async-start | bytes 2162688 | tf_op jit(solution)/shard_map/all_to_all | solution.py:241
  28.0 38.7 %collective-permute-start.4 = (bf16[8,256,128]{2,1,0:T(8,128)(2,1)}, bf16[8,256,128]{2,1,0:T(8,128)(2,1)}, u32[]{:S(2)}, u32[]{:S(2)}) collective-permute-start(bf16[8,256,128]{2,1,0:T(8,128)(2,1)} %collective-permute-done.2.refs_4_), channel_id=1, source_target_pairs={{0,112},{16,0},{32,16},{48,32},{64,48},{80,64},{96,80},{112,96},{1... | collective-permute-start | bytes 1572872 | tf_op jit(solution)/shard_map/ppermute | solution.py:144
  38.8 30.0 %collective-permute-start.5 = (bf16[8,256,128]{2,1,0:T(8,128)(2,1)S(1)}, bf16[8,256,128]{2,1,0:T(8,128)(2,1)S(1)}, u32[]{:S(2)}, u32[]{:S(2)}) collective-permute-start(bf16[8,256,128]{2,1,0:T(8,128)(2,1)S(1)} %collective-permute-done.3.refs_5_), channel_id=1, source_target_pairs={{0,16},{16,32},{32,48},{48,64},{64,80},{80,96},{96,112},{112,0},{1... | collective-permute-start | bytes 1572872 | tf_op jit(solution)/shard_map/ppermute | solution.py:142
  49.2 6.8 %copy-start.14 = (bf16[1,256,2048]{1,2,0:T(8,128)(2,1)S(1)}, bf16[1,256,2048]{1,2,0:T(8,128)(2,1)}, u32[]{:S(2)}) copy-start(bf16[1,256,2048]{1,2,0:T(8,128)(2,1)} %copy.28) | copy-start | bytes 3145732
  64.0 12.2 %copy-start.12 = (bf16[1,256,2048]{2,1,0:T(8,128)(2,1)S(1)}, bf16[1,256,2048]{2,1,0:T(8,128)(2,1)}, u32[]{:S(2)}) copy-start(bf16[1,256,2048]{2,1,0:T(8,128)(2,1)} %copy-done.11) | copy-start | bytes 3145732
  64.0 20.0 %collective-permute-start.10 = (bf16[8,256,128]{2,1,0:T(8,128)(2,1)}, bf16[8,256,128]{2,1,0:T(8,128)(2,1)S(1)}, u32[]{:S(2)}, u32[]{:S(2)}) collective-permute-start(bf16[8,256,128]{2,1,0:T(8,128)(2,1)} %collective-permute-done.2.refs_4_), channel_id=1, source_target_pairs={{0,128},{16,144},{32,160},{48,176},{64,192},{80,208},{96,224},{112... | collective-permute-start | bytes 1572872 | tf_op jit(solution)/shard_map/ppermute | solution.py:161
  65.4 26.8 %collective-permute-start.9 = (bf16[8,256,128]{2,1,0:T(8,128)(2,1)}, bf16[8,256,128]{2,1,0:T(8,128)(2,1)S(1)}, u32[]{:S(2)}, u32[]{:S(2)}) collective-permute-start(bf16[8,256,128]{2,1,0:T(8,128)(2,1)} %copy-done.9), channel_id=1, source_target_pairs={{0,128},{16,144},{32,160},{48,176},{64,192},{80,208},{96,224},{112... | collective-permute-start | bytes 1572872 | tf_op jit(solution)/shard_map/ppermute | solution.py:161
  66.7 26.8 %collective-permute-start.6 = (bf16[8,256,128]{2,1,0:T(8,128)(2,1)}, bf16[8,256,128]{2,1,0:T(8,128)(2,1)}, u32[]{:S(2)}, u32[]{:S(2)}) collective-permute-start(bf16[8,256,128]{2,1,0:T(8,128)(2,1)} %collective-permute-done.4.refs_6_), channel_id=1, source_target_pairs={{0,112},{16,0},{32,16},{48,32},{64,48},{80,64},{96,80},{112,96},{1... | collective-permute-start | bytes 1572872 | tf_op jit(solution)/shard_map/ppermute | solution.py:144
  68.8 26.0 %collective-permute-start.7 = (bf16[8,256,128]{2,1,0:T(8,128)(2,1)S(1)}, bf16[8,256,128]{2,1,0:T(8,128)(2,1)}, u32[]{:S(2)}, u32[]{:S(2)}) collective-permute-start(bf16[8,256,128]{2,1,0:T(8,128)(2,1)S(1)} %collective-permute-done.5.refs_7_), channel_id=1, source_target_pairs={{0,16},{16,32},{32,48},{48,64},{64,80},{80,96},{96,112},{112,0},{1... | collective-permute-start | bytes 1572872 | tf_op jit(solution)/shard_map/ppermute | solution.py:142
  82.7 58.9 %collective-permute-start.11 = (bf16[8,256,128]{2,1,0:T(8,128)(2,1)S(1)}, bf16[8,256,128]{2,1,0:T(8,128)(2,1)}, u32[]{:S(2)}, u32[]{:S(2)}) collective-permute-start(bf16[8,256,128]{2,1,0:T(8,128)(2,1)S(1)} %collective-permute-done.3.refs_5_), channel_id=1, source_target_pairs={{0,128},{16,144},{32,160},{48,176},{64,192},{80,208},{96,224},{112... | collective-permute-start | bytes 1572872 | tf_op jit(solution)/shard_map/ppermute | solution.py:161
  84.0 17.8 %copy-start.5 = (bf16[8,256,128]{2,1,0:T(8,128)(2,1)}, bf16[8,256,128]{2,1,0:T(8,128)(2,1)S(1)}, u32[]{:S(2)}) copy-start(bf16[8,256,128]{2,1,0:T(8,128)(2,1)S(1)} %collective-permute-done.10.refs_7_) | copy-start | bytes 1572868
  84.0 57.6 %collective-permute-start.12 = (bf16[8,256,128]{2,1,0:T(8,128)(2,1)}, bf16[8,256,128]{2,1,0:T(8,128)(2,1)}, u32[]{:S(2)}, u32[]{:S(2)}) collective-permute-start(bf16[8,256,128]{2,1,0:T(8,128)(2,1)} %collective-permute-done.4.refs_6_), channel_id=1, source_target_pairs={{0,128},{16,144},{32,160},{48,176},{64,192},{80,208},{96,224},{112... | collective-permute-start | bytes 1572872 | tf_op jit(solution)/shard_map/ppermute | solution.py:161
  92.2 9.6 %copy-start.7 = (bf16[8,256,128]{2,1,0:T(8,128)(2,1)}, bf16[8,256,128]{2,1,0:T(8,128)(2,1)S(1)}, u32[]{:S(2)}) copy-start(bf16[8,256,128]{2,1,0:T(8,128)(2,1)S(1)} %collective-permute-done.9.refs_6_) | copy-start | bytes 1572868
  92.2 68.3 %collective-permute-start.13 = (bf16[8,256,128]{2,1,0:T(8,128)(2,1)S(1)}, bf16[8,256,128]{2,1,0:T(8,128)(2,1)}, u32[]{:S(2)}, u32[]{:S(2)}) collective-permute-start(bf16[8,256,128]{2,1,0:T(8,128)(2,1)S(1)} %collective-permute-done.5.refs_7_), channel_id=1, source_target_pairs={{0,128},{16,144},{32,160},{48,176},{64,192},{80,208},{96,224},{112... | collective-permute-start | bytes 1572872 | tf_op jit(solution)/shard_map/ppermute | solution.py:161
  93.5 67.0 %collective-permute-start.14 = (bf16[8,256,128]{2,1,0:T(8,128)(2,1)}, bf16[8,256,128]{2,1,0:T(8,128)(2,1)}, u32[]{:S(2)}, u32[]{:S(2)}) collective-permute-start(bf16[8,256,128]{2,1,0:T(8,128)(2,1)} %collective-permute-done.6.refs_8_), channel_id=1, source_target_pairs={{0,128},{16,144},{32,160},{48,176},{64,192},{80,208},{96,224},{112... | collective-permute-start | bytes 1572872 | tf_op jit(solution)/shard_map/ppermute | solution.py:161
  94.9 74.1 %collective-permute-start.15 = (bf16[8,256,128]{2,1,0:T(8,128)(2,1)}, bf16[8,256,128]{2,1,0:T(8,128)(2,1)}, u32[]{:S(2)}, u32[]{:S(2)}) collective-permute-start(bf16[8,256,128]{2,1,0:T(8,128)(2,1)} %collective-permute-done.7.refs_9_), channel_id=1, source_target_pairs={{0,128},{16,144},{32,160},{48,176},{64,192},{80,208},{96,224},{112... | collective-permute-start | bytes 1572872 | tf_op jit(solution)/shard_map/ppermute | solution.py:161
  104.4 3.0 %copy-start.1 = (bf16[1,256,2048]{2,1,0:T(8,128)(2,1)S(1)}, bf16[1,256,2048]{2,1,0:T(8,128)(2,1)}, u32[]{:S(2)}) copy-start(bf16[1,256,2048]{2,1,0:T(8,128)(2,1)} %param.10) | copy-start | bytes 3145732
  107.4 1.0 copy-start.10
  118.7 1.3 copy-start.3
  122.6 19.0 %copy-start.6 = (bf16[8,256,128]{2,1,0:T(8,128)(2,1)S(1)}, bf16[8,256,128]{2,1,0:T(8,128)(2,1)}, u32[]{:S(2)}) copy-start(bf16[8,256,128]{2,1,0:T(8,128)(2,1)} %copy-done.5) | copy-start | bytes 1572868
  122.6 19.0 %copy-start.8 = (bf16[8,256,128]{2,1,0:T(8,128)(2,1)S(1)}, bf16[8,256,128]{2,1,0:T(8,128)(2,1)}, u32[]{:S(2)}) copy-start(bf16[8,256,128]{2,1,0:T(8,128)(2,1)} %copy-done.7) | copy-start | bytes 1572868
  140.3 1.3 copy-start.2
  159.2 1.3 copy-start.4
  169.0 5.3 %copy-start.13 = (f32[256,2048]{1,0:T(8,128)S(1)}, f32[256,2048]{1,0:T(8,128)}, u32[]{:S(2)}) copy-start(f32[256,2048]{1,0:T(8,128)} %copy.35) | copy-start | bytes 6291460
  169.0 5.3 %copy-start.15 = (bf16[1,256,2048]{2,1,0:T(8,128)(2,1)S(1)}, bf16[1,256,2048]{2,1,0:T(8,128)(2,1)}, u32[]{:S(2)}) copy-start(bf16[1,256,2048]{2,1,0:T(8,128)(2,1)} %param.14) | copy-start | bytes 3145732
